TPU v7x, 256 devices: a whole 4x4x8 slice. The times are simulated.
256 devices in a mesh: dp: 8 (over x, core), adapter: 32 (over y, z).
Axes of the slice: x: 4, y: 4, z: 8, core: 2. Of those that a mesh axis runs over, the one named last changes fastest.
Arguments:
- tokens: bfloat16 [32768, 8192], P(('dp', 'adapter')), may hold values from -6 to 6
- grad_out: bfloat16 [32768, 8192], P(('dp', 'adapter')), may hold values from -6 to 6
- down_panels: bfloat16 [64, 8192, 64], P('adapter'), may hold values from -0.0625 to 0.0625
- up_panels: bfloat16 [64, 64, 8192], P('adapter'), may hold values from -0.75 to 0.75
- seg_adapter: int32 [512], P(('dp', 'adapter')), may hold values from 0 to 63, as said below
Outputs:
- adapter_out: bfloat16 [32768, 8192], P(('dp', 'adapter'))
- grad_tokens: bfloat16 [32768, 8192], P(('dp', 'adapter'))
- grad_down: bfloat16 [64, 8192, 64], P('adapter', 'dp')
- grad_up: bfloat16 [64, 64, 8192], P('adapter', None, 'dp')
Inputs may be any that keep to these rules, and one draw needn't show every extreme that they name: `seg_adapter`: adapter a is held by index a // 2 of the adapter axis. A segment of the device at index j of the adapter axis names a holder (j + k) modulo the axis's size, with k from 0 to 3; the 2 segments of one device name different holders, and in every data group some holder is named by 4 segments.
All inputs are finite; a program needn't handle non-finite values.
Results may differ from a plain program's by a relative error of at most 0.0049.
Values may be sent and summed in bfloat16 or wider, within the bound.
No kernel may reach another device: no remote copies, remote signals or barrier semaphores. Data moves between devices by JAX's collectives and lax.ppermute only.
A program may use at most 128 MiB of HBM per device.

v0:
```python
import jax
import jax.numpy as jnp
from jax import lax
from jax.sharding import PartitionSpec as P

adapter_scale = 2.0


def shifted(value, axis, steps):
    count = lax.axis_size(axis)
    pairs = [(source, (source + steps) % count) for source in range(count)]
    return lax.ppermute(value, axis, pairs)


def slot_mask(selector, held_count, rank_size):
    picks = (
        selector.astype(jnp.float32) == jnp.arange(held_count, dtype=jnp.float32)[None, :]
    ).astype(jnp.float32)
    return jnp.repeat(picks, rank_size, axis=1)[:, None, :]


def on_device(tokens, grad_out, down_panels, up_panels, seg_adapter):
    groups = lax.axis_size("adapter")
    held_count, feat_width, rank_size = down_panels.shape
    segs_here = seg_adapter.shape[0]
    seg_rows = tokens.shape[0] // segs_here
    reach_count = 2 * segs_here
    position = lax.axis_index("adapter")
    owners_of = seg_adapter // held_count
    local_index = seg_adapter - owners_of * held_count
    distance = jnp.mod(owners_of - position, groups)
    placing = jnp.arange(reach_count, dtype=jnp.int32)[:, None] == distance[None, :]
    place_bf = placing.astype(jnp.bfloat16)
    selector = (jnp.sum(jnp.where(placing, local_index[None, :] + 1, 0), axis=1) - 1).astype(
        jnp.bfloat16
    )[:, None]
    down_cat = jnp.transpose(down_panels, (1, 0, 2)).reshape(feat_width, held_count * rank_size)
    up_weight_joined = up_panels.reshape(held_count * rank_size, feat_width)

    def pack_rows(token_rows):
        blocks = token_rows.reshape(segs_here, seg_rows, feat_width)
        return jnp.einsum(
            "ns,sjd->njd", place_bf, blocks, preferred_element_type=jnp.float32
        ).astype(jnp.bfloat16)

    def unpack(slot_rows):
        placed = jnp.einsum("ns,njd->sjd", place_bf, slot_rows, preferred_element_type=jnp.float32)
        return placed.astype(jnp.bfloat16).reshape(tokens.shape)

    sent_rows = pack_rows(tokens)
    sent_grads = pack_rows(grad_out)
    rows_list = [sent_rows[slot_index] for slot_index in range(reach_count)]
    grads_list = [sent_grads[slot_index] for slot_index in range(reach_count)]
    select_list = [selector[slot_index] for slot_index in range(reach_count)]
    for slot_index in range(1, reach_count):
        moved = shifted(
            (rows_list[slot_index], grads_list[slot_index], select_list[slot_index]),
            "adapter",
            slot_index,
        )
        rows_list[slot_index], grads_list[slot_index], select_list[slot_index] = moved
    arrived_rows = jnp.stack(rows_list)
    arrived_grads = jnp.stack(grads_list)
    arrived_select = jnp.stack(select_list)
    masking = slot_mask(arrived_select, held_count, rank_size)
    hidden_state = (
        jnp.einsum("njd,dc->njc", arrived_rows, down_cat, preferred_element_type=jnp.float32)
        * masking
    ).astype(jnp.bfloat16)
    projected_output = (
        adapter_scale
        * jnp.einsum(
            "qfs,su->qfu", hidden_state, up_weight_joined, preferred_element_type=jnp.float32
        )
    ).astype(jnp.bfloat16)
    hidden_gradient = adapter_scale * jnp.einsum(
        "njd,cd->njc", arrived_grads, up_weight_joined, preferred_element_type=jnp.float32
    )
    hidden_gradient = (hidden_gradient * masking).astype(jnp.bfloat16)
    grad_rows = jnp.einsum(
        "njc,dc->njd", hidden_gradient, down_cat, preferred_element_type=jnp.float32
    ).astype(jnp.bfloat16)
    down_sum = jnp.einsum(
        "njd,njc->dc", arrived_rows, hidden_gradient, preferred_element_type=jnp.float32
    )
    down_sum = jnp.transpose(down_sum.reshape(feat_width, held_count, rank_size), (1, 0, 2))
    up_weight_sum = adapter_scale * jnp.einsum(
        "njc,njd->cd", hidden_state, arrived_grads, preferred_element_type=jnp.float32
    )
    up_weight_sum = up_weight_sum.reshape(held_count, rank_size, feat_width)
    result_list = [projected_output[slot_index] for slot_index in range(reach_count)]
    back_list = [grad_rows[slot_index] for slot_index in range(reach_count)]
    for slot_index in range(1, reach_count):
        moved = shifted((result_list[slot_index], back_list[slot_index]), "adapter", -slot_index)
        result_list[slot_index], back_list[slot_index] = moved
    adapter_out = unpack(jnp.stack(result_list))
    grad_tokens = unpack(jnp.stack(back_list))
    grad_down, grad_up = (
        lax.psum_scatter(down_sum, "dp", scatter_dimension=1, tiled=True),
        lax.psum_scatter(up_weight_sum, "dp", scatter_dimension=2, tiled=True),
    )
    return (adapter_out, grad_tokens, grad_down.astype(jnp.bfloat16), grad_up.astype(jnp.bfloat16))


def solution(mesh):
    placed = (
        P(("dp", "adapter"), None),
        P(("dp", "adapter"), None),
        P("adapter", None, None),
        P("adapter", None, None),
        P(("dp", "adapter")),
    )
    return jax.shard_map(
        on_device,
        mesh=mesh,
        in_specs=placed,
        out_specs=(
            P(("dp", "adapter"), None),
            P(("dp", "adapter"), None),
            P("adapter", "dp", None),
            P("adapter", None, "dp"),
        ),
        check_vma=False,
    )
```

profile of v0, /device:TPU:71, one launch (start us, length us, event | category | flops | bytes accessed | tf_op | source)
XLA Modules:
  0.0 646.1 jit_solution(5786673812678965965)
XLA Ops:
  8.8 4.7 collective-permute-start.5
  14.7 5.8 convolution_convert_fusion.2
  20.5 10.0 %fusion.38 = (bf16[1,64,8192]{2,0,1:T(2,128)(2,1)}, bf16[1,64,8192]{2,0,1:T(2,128)(2,1)S(1)}, bf16[1,64,8192]{2,0,1:T(2,128)(2,1)S(1)}, bf16[1,64,8192]{2,0,1:T(2,128)(2,1)S(1)}) fusion(bf16[4,64,8192]{2,0,1:T(4,128)(2,1)S(1)} %convolution_convert_fusion.2), kind=kLoop, calls=%fused_computation.67 | loop fusion | bytes 8388608 | tf_op jit(solution)/shard_map/slice | solution.py:52
  32.0 2.1 copy.117
  34.1 2.9 collective-permute-start.1
  37.0 3.8 convolution_convert_fusion.1
  40.8 10.0 %fusion.36 = (bf16[1,64,8192]{2,0,1:T(2,128)(2,1)}, bf16[1,64,8192]{2,0,1:T(2,128)(2,1)S(1)}, bf16[1,64,8192]{2,0,1:T(2,128)(2,1)S(1)}, bf16[1,64,8192]{2,0,1:T(2,128)(2,1)S(1)}) fusion(bf16[4,64,8192]{2,0,1:T(4,128)(2,1)S(1)} %convolution_convert_fusion.1), kind=kLoop, calls=%fused_computation.65 | loop fusion | bytes 8388608 | tf_op jit(solution)/shard_map/slice | solution.py:53
  50.9 2.1 copy.116
  54.1 2.1 copy.114
  56.2 2.1 copy.115
  58.4 3.8 collective-permute-start.2
  62.9 5.1 collective-permute-start.11
  68.1 2.5 maximum_convert_fusion
  70.8 3.5 copy.56
  74.4 6.7 %collective-permute-done.1 = bf16[64,8192]{1,0:T(8,128)(2,1)} collective-permute-done((bf16[64,8192]{1,0:T(8,128)(2,1)}, bf16[64,8192]{1,0:T(8,128)(2,1)}, u32[]{:S(2)}, u32[]{:S(2)}) %collective-permute-start.1) | collective-permute-done | bytes 1048608 | tf_op jit(solution)/shard_map/ppermute | solution.py:12
  81.1 3.5 copy.57
  84.6 77.9 %collective-permute-done.2 = bf16[64,8192]{1,0:T(8,128)(2,1)} collective-permute-done((bf16[64,8192]{1,0:T(8,128)(2,1)}, bf16[64,8192]{1,0:T(8,128)(2,1)}, u32[]{:S(2)}, u32[]{:S(2)}) %collective-permute-start.2) | collective-permute-done | bytes 1048608 | tf_op jit(solution)/shard_map/ppermute | solution.py:12
  162.5 3.5 copy.58
  166.1 24.1 %collective-permute-done.9 = bf16[64,8192]{1,0:T(8,128)(2,1)} collective-permute-done((bf16[64,8192]{1,0:T(8,128)(2,1)}, bf16[64,8192]{1,0:T(8,128)(2,1)}, u32[]{:S(2)}, u32[]{:S(2)}) %collective-permute-start.9) | collective-permute-done | bytes 1048608 | tf_op jit(solution)/shard_map/ppermute | solution.py:12
  190.1 3.7 copy.64
  193.8 22.1 %collective-permute-done.10 = bf16[64,8192]{1,0:T(8,128)(2,1)} collective-permute-done((bf16[64,8192]{1,0:T(8,128)(2,1)}, bf16[64,8192]{1,0:T(8,128)(2,1)}, u32[]{:S(2)}, u32[]{:S(2)}) %collective-permute-start.10) | collective-permute-done | bytes 1048608 | tf_op jit(solution)/shard_map/ppermute | solution.py:12
  215.9 3.5 copy.65
  219.5 77.9 %collective-permute-done.11 = bf16[64,8192]{1,0:T(8,128)(2,1)} collective-permute-done((bf16[64,8192]{1,0:T(8,128)(2,1)S(1)}, bf16[64,8192]{1,0:T(8,128)(2,1)}, u32[]{:S(2)}, u32[]{:S(2)}) %collective-permute-start.11) | collective-permute-done | bytes 1048608 | tf_op jit(solution)/shard_map/ppermute | solution.py:12
  297.3 3.5 copy.66
  300.9 10.2 %pad_maximum_fusion.2 = bf16[4,64,8192]{2,0,1:T(4,128)(2,1)S(1)} fusion(bf16[1,64,8192]{2,0,1:T(2,128)(2,1)S(1)} %copy.66, bf16[1,64,8192]{2,0,1:T(2,128)(2,1)S(1)} %copy.65, bf16[1,64,8192]{2,0,1:T(2,128)(2,1)S(1)} %copy.64, bf16[1,64,8192]{2,0,1:T(2,128)(2,1)S(1)} %copy-done.5), kind=kLoop, calls=%fused_computation.11 | loop fusion | flops 16777216 | bytes 8388608 | tf_op jit(solution)/shard_map/stack | solution.py:63
  311.2 4.8 fusion.19
  316.0 9.8 %pad_maximum_fusion = bf16[4,64,8192]{2,0,1:T(4,128)(2,1)S(1)} fusion(bf16[1,64,8192]{2,0,1:T(2,128)(2,1)S(1)} %copy.58, bf16[1,64,8192]{2,0,1:T(2,128)(2,1)S(1)} %copy.57, bf16[1,64,8192]{2,0,1:T(2,128)(2,1)S(1)} %copy.56, bf16[1,64,8192]{2,0,1:T(2,128)(2,1)S(1)} %copy-done.4), kind=kLoop, calls=%fused_computation.9 | loop fusion | flops 16777216 | bytes 8388608 | tf_op jit(solution)/shard_map/stack | solution.py:62
  325.9 6.9 %fusion.7 = f32[8192,128,1]{0,1,2:T(8,128)} fusion(bf16[4,64,128]{2,1,0:T(8,128)(2,1)S(1)} %fusion.19, bf16[4,64,8192]{2,0,1:T(4,128)(2,1)S(1)} %pad_maximum_fusion), kind=kOutput, calls=%fused_computation.18 | convolution fusion | flops 536870912 | bytes 8454144 | tf_op jit(solution)/shard_map/njd,njc->dc/dot_general | solution.py:83
  333.0 7.7 %fusion.22 = bf16[4,64,128]{2,1,0:T(8,128)(2,1)S(1)} fusion(bf16[8192,128,1]{0,1,2:T(8,128)(2,1)} %bitcast.88, bf16[4,64,8192]{2,0,1:T(4,128)(2,1)} %copy-done.1, f32[4,128]{1,0:T(4,128)S(1)} %mul.40), kind=kOutput, calls=%fused_computation.27 | convolution fusion | flops 536936448 | bytes 6359040 | tf_op jit(solution)/shard_map/njd,dc->njc/dot_general | solution.py:67
  340.8 7.0 %fusion.1 = f32[128,8192]{1,0:T(8,128)} fusion(bf16[4,64,128]{2,1,0:T(8,128)(2,1)S(1)} %fusion.22, bf16[4,64,8192]{2,0,1:T(4,128)(2,1)S(1)} %copy-done.3), kind=kOutput, calls=%fused_computation.6 | convolution fusion | flops 537919488 | bytes 8454144 | tf_op jit(solution)/shard_map/njc,njd->cd/dot_general | solution.py:87
  347.8 1.2 fusion
  349.5 3.4 collective-permute-start.8
  352.9 7.2 %collective-permute-start.7 = (bf16[64,8192]{1,0:T(8,128)(2,1)S(1)}, bf16[64,8192]{1,0:T(8,128)(2,1)S(1)}, u32[]{:S(2)}, u32[]{:S(2)}) collective-permute-start(bf16[64,8192]{1,0:T(8,128)(2,1)S(1)} %get-tuple-element.16), channel_id=1, source_target_pairs={{0,30},{1,31},{2,0},{3,1},{4,2},{5,3},{6,4},{7,5},{8,6},{9,7},{10,... | collective-permute-start | bytes 3145736 | tf_op jit(solution)/shard_map/ppermute | solution.py:12
  362.1 3.1 collective-permute-start.14
  365.2 2.6 collective-permute-start.13
  367.8 43.1 %collective-permute-done.8 = bf16[64,8192]{1,0:T(8,128)(2,1)S(1)} collective-permute-done((bf16[64,8192]{1,0:T(8,128)(2,1)S(1)}, bf16[64,8192]{1,0:T(8,128)(2,1)S(1)}, u32[]{:S(2)}, u32[]{:S(2)}) %collective-permute-start.8) | collective-permute-done | bytes 1048608 | tf_op jit(solution)/shard_map/ppermute | solution.py:12
  410.9 11.5 %collective-permute-start.12 = (bf16[64,8192]{1,0:T(8,128)(2,1)S(1)}, bf16[64,8192]{1,0:T(8,128)(2,1)S(1)}, u32[]{:S(2)}, u32[]{:S(2)}) collective-permute-start(bf16[64,8192]{1,0:T(8,128)(2,1)S(1)} %get-tuple-element.9), channel_id=1, source_target_pairs={{0,31},{1,0},{2,1},{3,2},{4,3},{5,4},{6,5},{7,6},{8,7},{9,8},{10,9... | collective-permute-start | bytes 3145736 | tf_op jit(solution)/shard_map/ppermute | solution.py:12
  422.5 23.0 %collective-permute-done.7 = bf16[64,8192]{1,0:T(8,128)(2,1)S(1)} collective-permute-done((bf16[64,8192]{1,0:T(8,128)(2,1)S(1)}, bf16[64,8192]{1,0:T(8,128)(2,1)S(1)}, u32[]{:S(2)}, u32[]{:S(2)}) %collective-permute-start.7) | collective-permute-done | bytes 1048608 | tf_op jit(solution)/shard_map/ppermute | solution.py:12
  445.5 53.8 %collective-permute-done.6 = bf16[64,8192]{1,0:T(8,128)(2,1)S(1)} collective-permute-done((bf16[64,8192]{1,0:T(8,128)(2,1)S(1)}, bf16[64,8192]{1,0:T(8,128)(2,1)S(1)}, u32[]{:S(2)}, u32[]{:S(2)}) %collective-permute-start.6) | collective-permute-done | bytes 1048608 | tf_op jit(solution)/shard_map/ppermute | solution.py:12
  499.9 4.0 convolution_convert_fusion.4
  503.9 2.5 copy.62
  506.4 40.9 %collective-permute-done.14 = bf16[64,8192]{1,0:T(8,128)(2,1)S(1)} collective-permute-done((bf16[64,8192]{1,0:T(8,128)(2,1)S(1)}, bf16[64,8192]{1,0:T(8,128)(2,1)S(1)}, u32[]{:S(2)}, u32[]{:S(2)}) %collective-permute-start.14) | collective-permute-done | bytes 1048608 | tf_op jit(solution)/shard_map/ppermute | solution.py:12
  547.2 33.1 %collective-permute-done.13 = bf16[64,8192]{1,0:T(8,128)(2,1)S(1)} collective-permute-done((bf16[64,8192]{1,0:T(8,128)(2,1)S(1)}, bf16[64,8192]{1,0:T(8,128)(2,1)S(1)}, u32[]{:S(2)}, u32[]{:S(2)}) %collective-permute-start.13) | collective-permute-done | bytes 1048608 | tf_op jit(solution)/shard_map/ppermute | solution.py:12
  580.3 48.1 %collective-permute-done.12 = bf16[64,8192]{1,0:T(8,128)(2,1)S(1)} collective-permute-done((bf16[64,8192]{1,0:T(8,128)(2,1)S(1)}, bf16[64,8192]{1,0:T(8,128)(2,1)S(1)}, u32[]{:S(2)}, u32[]{:S(2)}) %collective-permute-start.12) | collective-permute-done | bytes 1048608 | tf_op jit(solution)/shard_map/ppermute | solution.py:12
  629.0 4.0 convolution_convert_fusion.3
  633.0 2.5 copy.70
  635.5 1.8 convert_element_type.56
  637.2 1.8 convert_element_type.57
  (50 shorter events, 10.3 us)
Async XLA Ops:
  7.2 304.0 %copy-start = (bf16[2,64,8192]{2,1,0:T(8,128)(2,1)S(1)}, bf16[2,64,8192]{2,1,0:T(8,128)(2,1)}, u32[]{:S(2)}) copy-start(bf16[2,64,8192]{2,1,0:T(8,128)(2,1)} %param.8) | copy-start | bytes 6291460
  7.2 628.3 %reduce-scatter.3.cloned.1.call-start = ((), (), s32[]{:S(2)}) async-start(), calls=%async_computation.2 | async-start | bytes 4718592 | tf_op jit(solution)/shard_map/reduce_scatter | solution.py:99
  8.8 49.6 %collective-permute-start.5 = (bf16[1]{0:T(256)(128)(2,1)}, bf16[1]{0:T(256)(128)(2,1)}, u32[]{:S(2)}, u32[]{:S(2)}) collective-permute-start(bf16[1]{0:T(256)(128)(2,1)} %get-tuple-element.23), channel_id=1, source_target_pairs={{0,3},{1,4},{2,5},{3,6},{4,7},{5,8},{6,9},{7,10},{8,11},{9,12},{10... | collective-permute-start | bytes 14 | tf_op jit(solution)/shard_map/ppermute | solution.py:12
  13.5 48.7 %collective-permute-start.4 = (bf16[1]{0:T(256)(128)(2,1)}, bf16[1]{0:T(256)(128)(2,1)}, u32[]{:S(2)}, u32[]{:S(2)}) collective-permute-start(bf16[1]{0:T(256)(128)(2,1)} %get-tuple-element.24), channel_id=1, source_target_pairs={{0,2},{1,3},{2,4},{3,5},{4,6},{5,7},{6,8},{7,9},{8,10},{9,11},{10,... | collective-permute-start | bytes 14 | tf_op jit(solution)/shard_map/ppermute | solution.py:12
  14.7 48.2 %collective-permute-start.3 = (bf16[1]{0:T(256)(128)(2,1)}, bf16[1]{0:T(256)(128)(2,1)}, u32[]{:S(2)}, u32[]{:S(2)}) collective-permute-start(bf16[1]{0:T(256)(128)(2,1)} %get-tuple-element.25), channel_id=1, source_target_pairs={{0,1},{1,2},{2,3},{3,4},{4,5},{5,6},{6,7},{7,8},{8,9},{9,10},{10,1... | collective-permute-start | bytes 14 | tf_op jit(solution)/shard_map/ppermute | solution.py:12
  30.5 6.5 %copy-start.8 = (bf16[128,8192]{1,0:T(8,128)(2,1)S(1)}, bf16[128,8192]{1,0:T(8,128)(2,1)}, u32[]{:S(2)}) copy-start(bf16[128,8192]{1,0:T(8,128)(2,1)} %param.6) | copy-start | bytes 6291460
  31.6 31.3 %collective-permute-start = (bf16[64,8192]{1,0:T(8,128)(2,1)S(1)}, bf16[64,8192]{1,0:T(8,128)(2,1)S(1)}, u32[]{:S(2)}, u32[]{:S(2)}) collective-permute-start(bf16[64,8192]{1,0:T(8,128)(2,1)S(1)} %bitcast.92), channel_id=1, source_target_pairs={{0,1},{1,2},{2,3},{3,4},{4,5},{5,6},{6,7},{7,8},{8,9},{9,10},{10,1... | collective-permute-start | bytes 3145736 | tf_op jit(solution)/shard_map/ppermute | solution.py:12
  34.1 46.9 %collective-permute-start.1 = (bf16[64,8192]{1,0:T(8,128)(2,1)}, bf16[64,8192]{1,0:T(8,128)(2,1)}, u32[]{:S(2)}, u32[]{:S(2)}) collective-permute-start(bf16[64,8192]{1,0:T(8,128)(2,1)} %bitcast.80), channel_id=1, source_target_pairs={{0,2},{1,3},{2,4},{3,5},{4,6},{5,7},{6,8},{7,9},{8,10},{9,11},{10,... | collective-permute-start | bytes 3145736 | tf_op jit(solution)/shard_map/ppermute | solution.py:12
  58.4 104.1 %collective-permute-start.2 = (bf16[64,8192]{1,0:T(8,128)(2,1)}, bf16[64,8192]{1,0:T(8,128)(2,1)}, u32[]{:S(2)}, u32[]{:S(2)}) collective-permute-start(bf16[64,8192]{1,0:T(8,128)(2,1)} %bitcast.79), channel_id=1, source_target_pairs={{0,3},{1,4},{2,5},{3,6},{4,7},{5,8},{6,9},{7,10},{8,11},{9,12},{10... | collective-permute-start | bytes 3145736 | tf_op jit(solution)/shard_map/ppermute | solution.py:12
  62.1 128.0 %collective-permute-start.9 = (bf16[64,8192]{1,0:T(8,128)(2,1)}, bf16[64,8192]{1,0:T(8,128)(2,1)}, u32[]{:S(2)}, u32[]{:S(2)}) collective-permute-start(bf16[64,8192]{1,0:T(8,128)(2,1)} %bitcast.78), channel_id=1, source_target_pairs={{0,1},{1,2},{2,3},{3,4},{4,5},{5,6},{6,7},{7,8},{8,9},{9,10},{10,1... | collective-permute-start | bytes 3145736 | tf_op jit(solution)/shard_map/ppermute | solution.py:12
  62.9 153.0 %collective-permute-start.10 = (bf16[64,8192]{1,0:T(8,128)(2,1)}, bf16[64,8192]{1,0:T(8,128)(2,1)}, u32[]{:S(2)}, u32[]{:S(2)}) collective-permute-start(bf16[64,8192]{1,0:T(8,128)(2,1)} %bitcast.77), channel_id=1, source_target_pairs={{0,2},{1,3},{2,4},{3,5},{4,6},{5,7},{6,8},{7,9},{8,10},{9,11},{10,... | collective-permute-start | bytes 3145736 | tf_op jit(solution)/shard_map/ppermute | solution.py:12
  62.9 5.1 copy-start.7
  62.9 234.4 %collective-permute-start.11 = (bf16[64,8192]{1,0:T(8,128)(2,1)S(1)}, bf16[64,8192]{1,0:T(8,128)(2,1)}, u32[]{:S(2)}, u32[]{:S(2)}) collective-permute-start(bf16[64,8192]{1,0:T(8,128)(2,1)S(1)} %bitcast.90), channel_id=1, source_target_pairs={{0,3},{1,4},{2,5},{3,6},{4,7},{5,8},{6,9},{7,10},{8,11},{9,12},{10... | collective-permute-start | bytes 3145736 | tf_op jit(solution)/shard_map/ppermute | solution.py:12
  190.1 110.8 %copy-start.5 = (bf16[1,64,8192]{2,0,1:T(2,128)(2,1)S(1)}, bf16[1,64,8192]{2,0,1:T(2,128)(2,1)}, u32[]{:S(2)}) copy-start(bf16[1,64,8192]{2,0,1:T(2,128)(2,1)} %get-tuple-element.10) | copy-start | bytes 3145732
  311.2 4.9 copy-start.2
  311.2 4.9 copy-start.4
  325.9 6.9 %copy-start.1 = (bf16[4,64,8192]{2,0,1:T(4,128)(2,1)}, bf16[4,64,8192]{2,0,1:T(4,128)(2,1)S(1)}, u32[]{:S(2)}) copy-start(bf16[4,64,8192]{2,0,1:T(4,128)(2,1)S(1)} %pad_maximum_fusion) | copy-start | bytes 12582916
  332.8 304.4 %reduce-scatter.5.cloned.1.call-start = ((), (), s32[]{:S(2)}) async-start(), calls=%async_computation.3 | async-start | bytes 4718592 | tf_op jit(solution)/shard_map/reduce_scatter | solution.py:100
  333.0 7.8 %copy-start.3 = (bf16[4,64,8192]{2,0,1:T(4,128)(2,1)S(1)}, bf16[4,64,8192]{2,0,1:T(4,128)(2,1)}, u32[]{:S(2)}) copy-start(bf16[4,64,8192]{2,0,1:T(4,128)(2,1)} %copy-done.2) | copy-start | bytes 12582916
  349.0 11.4 %copy-start.6 = (bf16[2,8192,64]{1,2,0:T(8,128)(2,1)S(1)}, bf16[2,8192,64]{1,2,0:T(8,128)(2,1)}, u32[]{:S(2)}) copy-start(bf16[2,8192,64]{1,2,0:T(8,128)(2,1)} %param.7) | copy-start | bytes 6291460
  349.5 61.5 %collective-permute-start.8 = (bf16[64,8192]{1,0:T(8,128)(2,1)S(1)}, bf16[64,8192]{1,0:T(8,128)(2,1)S(1)}, u32[]{:S(2)}, u32[]{:S(2)}) collective-permute-start(bf16[64,8192]{1,0:T(8,128)(2,1)S(1)} %get-tuple-element.15), channel_id=1, source_target_pairs={{0,29},{1,30},{2,31},{3,0},{4,1},{5,2},{6,3},{7,4},{8,5},{9,6},{10... | collective-permute-start | bytes 3145736 | tf_op jit(solution)/shard_map/ppermute | solution.py:12
  352.9 92.6 %collective-permute-start.7 = (bf16[64,8192]{1,0:T(8,128)(2,1)S(1)}, bf16[64,8192]{1,0:T(8,128)(2,1)S(1)}, u32[]{:S(2)}, u32[]{:S(2)}) collective-permute-start(bf16[64,8192]{1,0:T(8,128)(2,1)S(1)} %get-tuple-element.16), channel_id=1, source_target_pairs={{0,30},{1,31},{2,0},{3,1},{4,2},{5,3},{6,4},{7,5},{8,6},{9,7},{10,... | collective-permute-start | bytes 3145736 | tf_op jit(solution)/shard_map/ppermute | solution.py:12
  360.1 139.2 %collective-permute-start.6 = (bf16[64,8192]{1,0:T(8,128)(2,1)S(1)}, bf16[64,8192]{1,0:T(8,128)(2,1)S(1)}, u32[]{:S(2)}, u32[]{:S(2)}) collective-permute-start(bf16[64,8192]{1,0:T(8,128)(2,1)S(1)} %get-tuple-element.17), channel_id=1, source_target_pairs={{0,31},{1,0},{2,1},{3,2},{4,3},{5,4},{6,5},{7,6},{8,7},{9,8},{10,9... | collective-permute-start | bytes 3145736 | tf_op jit(solution)/shard_map/ppermute | solution.py:12
  362.1 185.1 %collective-permute-start.14 = (bf16[64,8192]{1,0:T(8,128)(2,1)S(1)}, bf16[64,8192]{1,0:T(8,128)(2,1)S(1)}, u32[]{:S(2)}, u32[]{:S(2)}) collective-permute-start(bf16[64,8192]{1,0:T(8,128)(2,1)S(1)} %get-tuple-element.7), channel_id=1, source_target_pairs={{0,29},{1,30},{2,31},{3,0},{4,1},{5,2},{6,3},{7,4},{8,5},{9,6},{10... | collective-permute-start | bytes 3145736 | tf_op jit(solution)/shard_map/ppermute | solution.py:12
  365.2 215.2 %collective-permute-start.13 = (bf16[64,8192]{1,0:T(8,128)(2,1)S(1)}, bf16[64,8192]{1,0:T(8,128)(2,1)S(1)}, u32[]{:S(2)}, u32[]{:S(2)}) collective-permute-start(bf16[64,8192]{1,0:T(8,128)(2,1)S(1)} %get-tuple-element.8), channel_id=1, source_target_pairs={{0,30},{1,31},{2,0},{3,1},{4,2},{5,3},{6,4},{7,5},{8,6},{9,7},{10,... | collective-permute-start | bytes 3145736 | tf_op jit(solution)/shard_map/ppermute | solution.py:12
  410.9 217.5 %collective-permute-start.12 = (bf16[64,8192]{1,0:T(8,128)(2,1)S(1)}, bf16[64,8192]{1,0:T(8,128)(2,1)S(1)}, u32[]{:S(2)}, u32[]{:S(2)}) collective-permute-start(bf16[64,8192]{1,0:T(8,128)(2,1)S(1)} %get-tuple-element.9), channel_id=1, source_target_pairs={{0,31},{1,0},{2,1},{3,2},{4,3},{5,4},{6,5},{7,6},{8,7},{9,8},{10,9... | collective-permute-start | bytes 3145736 | tf_op jit(solution)/shard_map/ppermute | solution.py:12
Sparse Core Ops, SparseCore 0:
  332.9 46.9 reduce-scatter.2
  382.5 40.0 reduce-scatter.4
where the time goes:
time: 653 us; the launch traced here: 646 us
  waiting for transfers between devices  451 us (69%)
  local copies, waits for them, and re-layouts  58.9 us (9%)
  starting transfers between devices  47.2 us (7%)
  matrix products  46.5 us (7%)
  other arithmetic  28.2 us (4%)
  between operations  14.6 us (2%)
    ppermute x15, waiting for transfers between devices, shifted(): return lax.ppermute(value, axis, pairs)  451 us
    ppermute x15, starting transfers between devices, shifted(): return lax.ppermute(value, axis, pairs)  46.9 us
  transfers between devices with their start and end apart: 17, of which 11 were waited for; matrix products, arithmetic and copies ran while one was open for 15% of the time, Pallas kernels for 0%

commit v1 on v0

v1 whole, which is shorter than its diff:
```python
import jax
import jax.numpy as jnp
from jax import lax
from jax.sharding import PartitionSpec as P


adapter_scale = 2.0


def shifted(value, axis, steps):
    count = lax.axis_size(axis)
    pairs = [(source, (source + steps) % count) for source in range(count)]
    return lax.ppermute(value, axis, pairs)


def pick(selector, choices, fallback):
    out = fallback
    for index, choice in enumerate(choices):
        out = jnp.where(selector == index, choice, out)
    return out


def on_device(tokens, grad_out, down_panels, up_panels, seg_adapter):
    groups = lax.axis_size("adapter")
    held_count, feat_width, rank_size = down_panels.shape
    segs_here = seg_adapter.shape[0]
    seg_rows = tokens.shape[0] // segs_here
    reach_count = 2 * segs_here
    position = lax.axis_index("adapter")
    owners_of = seg_adapter // held_count
    local_index = seg_adapter - owners_of * held_count
    distance = jnp.mod(owners_of - position, groups)

    token_blocks = tokens.reshape(segs_here, seg_rows, feat_width)
    grad_blocks = grad_out.reshape(segs_here, seg_rows, feat_width)

    def slot_of(blocks, slot_index):
        out = jnp.zeros_like(blocks[0])
        for seg in range(segs_here):
            out = jnp.where(distance[seg] == slot_index, blocks[seg], out)
        return out

    def selector_of(slot_index):
        sel = jnp.int32(-1)
        for seg in range(segs_here):
            sel = jnp.where(distance[seg] == slot_index, local_index[seg], sel)
        return sel.reshape(1)

    sel_list = [selector_of(k) for k in range(reach_count)]
    arrived_sel = [sel_list[0]] + [
        shifted(sel_list[k], "adapter", k) for k in range(1, reach_count)
    ]

    rows_list = [slot_of(token_blocks, k) for k in range(reach_count)]
    grads_list = [slot_of(grad_blocks, k) for k in range(reach_count)]
    for k in range(1, reach_count):
        rows_list[k], grads_list[k] = shifted((rows_list[k], grads_list[k]), "adapter", k)

    down_back = [None] * reach_count
    up_back = [None] * reach_count
    for k in range(1, reach_count):
        sel = arrived_sel[k][0]
        down_pick = pick(sel, [down_panels[i] for i in range(held_count)], down_panels[0])
        up_pick = pick(sel, [up_panels[i] for i in range(held_count)], up_panels[0])
        down_back[k], up_back[k] = shifted((down_pick, up_pick), "adapter", -k)

    outs = []
    backs = []
    for seg in range(segs_here):
        own_down = pick(local_index[seg], [down_panels[i] for i in range(held_count)], down_panels[0])
        own_up = pick(local_index[seg], [up_panels[i] for i in range(held_count)], up_panels[0])
        seg_down = own_down
        seg_up = own_up
        for k in range(1, reach_count):
            seg_down = jnp.where(distance[seg] == k, down_back[k], seg_down)
            seg_up = jnp.where(distance[seg] == k, up_back[k], seg_up)
        hidden = jnp.dot(token_blocks[seg], seg_down, preferred_element_type=jnp.float32).astype(
            jnp.bfloat16
        )
        outs.append(
            (adapter_scale * jnp.dot(hidden, seg_up, preferred_element_type=jnp.float32)).astype(
                jnp.bfloat16
            )
        )
        hidden_grad = (
            adapter_scale
            * lax.dot_general(
                grad_blocks[seg], seg_up, (((1,), (1,)), ((), ())), preferred_element_type=jnp.float32
            )
        ).astype(jnp.bfloat16)
        backs.append(
            lax.dot_general(
                hidden_grad, seg_down, (((1,), (1,)), ((), ())), preferred_element_type=jnp.float32
            ).astype(jnp.bfloat16)
        )
    adapter_out = jnp.concatenate(outs, axis=0)
    grad_tokens = jnp.concatenate(backs, axis=0)

    arrived_rows = jnp.stack(rows_list)
    arrived_grads = jnp.stack(grads_list)
    arrived_select = jnp.concatenate(arrived_sel).astype(jnp.float32)
    picks = (arrived_select[:, None] == jnp.arange(held_count, dtype=jnp.float32)[None, :]).astype(
        jnp.float32
    )
    masking = jnp.repeat(picks, rank_size, axis=1)[:, None, :]
    down_cat = jnp.transpose(down_panels, (1, 0, 2)).reshape(feat_width, held_count * rank_size)
    up_weight_joined = up_panels.reshape(held_count * rank_size, feat_width)
    hidden_state = (
        jnp.einsum("njd,dc->njc", arrived_rows, down_cat, preferred_element_type=jnp.float32)
        * masking
    ).astype(jnp.bfloat16)
    hidden_gradient = adapter_scale * jnp.einsum(
        "njd,cd->njc", arrived_grads, up_weight_joined, preferred_element_type=jnp.float32
    )
    hidden_gradient = (hidden_gradient * masking).astype(jnp.bfloat16)
    down_sum = jnp.einsum(
        "njd,njc->dc", arrived_rows, hidden_gradient, preferred_element_type=jnp.float32
    )
    down_sum = jnp.transpose(down_sum.reshape(feat_width, held_count, rank_size), (1, 0, 2))
    up_weight_sum = adapter_scale * jnp.einsum(
        "njc,njd->cd", hidden_state, arrived_grads, preferred_element_type=jnp.float32
    )
    up_weight_sum = up_weight_sum.reshape(held_count, rank_size, feat_width)
    grad_down, grad_up = (
        lax.psum_scatter(down_sum, "dp", scatter_dimension=1, tiled=True),
        lax.psum_scatter(up_weight_sum, "dp", scatter_dimension=2, tiled=True),
    )
    return (adapter_out, grad_tokens, grad_down.astype(jnp.bfloat16), grad_up.astype(jnp.bfloat16))


def solution(mesh):
    placed = (
        P(("dp", "adapter"), None),
        P(("dp", "adapter"), None),
        P("adapter", None, None),
        P("adapter", None, None),
        P(("dp", "adapter")),
    )
    return jax.shard_map(
        on_device,
        mesh=mesh,
        in_specs=placed,
        out_specs=(
            P(("dp", "adapter"), None),
            P(("dp", "adapter"), None),
            P("adapter", "dp", None),
            P("adapter", None, "dp"),
        ),
        check_vma=False,
    )
```

time: 653 us -> 616 us (0.943)
  local copies, waits for them, and re-layouts: 58.9 us -> 3.99 us
  waiting for transfers between devices: 451 us -> 490 us
  matrix products: 46.5 us -> 32.3 us
  starting transfers between devices: 47.2 us -> 33.6 us
  between operations: 14.6 us -> 27.6 us
  other arithmetic: 28.2 us -> 21.2 us
    ppermute x15, waiting for transfers between devices: 451 us -> 490 us  [shifted(): return lax.ppermute(value, axis, pairs)]
    another operation x6 -> x0, local copies, waits for them, and re-layouts: 21.4 us -> none  [the longest x3 10.8 us: on_device(): arrived_grads = jnp.stack(grads_list)]
    slice x5 -> x2, local copies, waits for them, and re-layouts: 21.6 us -> 1.23 us  [the longest x1 0.65 us: selector_of(): sel = jnp.where(distance[seg] == slot_index, local_index[seg], sel)]
    dot_general x8 -> x4, matrix products: 32.6 us -> 15.1 us  [the longest x2 7.62 us: on_device(): jnp.dot(hidden, seg_up, preferred_element_type=jnp.float32)]
    ppermute x15, starting transfers between devices: 46.9 us -> 33.5 us  [shifted(): return lax.ppermute(value, axis, pairs)]
    unnamed x24 -> x20, local copies, waits for them, and re-layouts: 10.8 us -> 2.6 us
    another operation x1, other arithmetic: 10.2 us -> 2.16 us  [on_device(): arrived_grads = jnp.stack(grads_list)]
  transfers between devices with their start and end apart: 17 -> 17, of which waited for: 11 -> 12; matrix products, arithmetic and copies ran while one was open for 15% -> 7% of each run, Pallas kernels for 0% -> 0%
where the time goes in v1:
time: 616 us; the launch traced here: 609 us
  waiting for transfers between devices  490 us (80%)
  starting transfers between devices  33.6 us (5%)
  matrix products  32.3 us (5%)
  between operations  27.6 us (4%)
  other arithmetic  21.2 us (3%)
    ppermute x15, waiting for transfers between devices, shifted(): return lax.ppermute(value, axis, pairs)  490 us
    ppermute x15, starting transfers between devices, shifted(): return lax.ppermute(value, axis, pairs)  33.5 us
  transfers between devices with their start and end apart: 17, of which 12 were waited for; matrix products, arithmetic and copies ran while one was open for 7% of the time, Pallas kernels for 0%

profile of v1, /device:TPU:71, one launch (start us, length us, event | category | flops | bytes accessed | tf_op | source)
XLA Modules:
  0.0 609.1 jit_solution(18023021588040939258)
XLA Ops:
  7.2 0.7 multiply_subtract_fusion
  7.9 0.6 fusion.37
  8.5 0.6 fusion.36
  11.7 5.5 collective-permute-start
  19.8 2.0 collective-permute-start.2
  24.4 0.8 collective-permute-start.4
  26.5 3.3 select_bitcast_fusion.1
  29.8 0.3 collective-permute-start.9
  30.1 2.4 collective-permute-start.10
  32.6 2.2 select_bitcast_fusion
  34.7 3.8 collective-permute-start.11
  38.5 0.7 collective-permute-start.12
  39.2 12.3 %collective-permute-done.9 = bf16[64,8192]{1,0:T(8,128)(2,1)S(1)} collective-permute-done((bf16[64,8192]{1,0:T(8,128)(2,1)S(1)}, bf16[64,8192]{1,0:T(8,128)(2,1)S(1)}, u32[]{:S(2)}, u32[]{:S(2)}) %collective-permute-start.9) | collective-permute-done | bytes 1048608 | tf_op jit(solution)/shard_map/ppermute | solution.py:13
  51.6 1.0 copy-done.9
  52.6 3.5 collective-permute-start.14
  57.4 1.9 add_convert_fusion
  59.3 0.1 fusion.28
  59.4 0.1 mul.52
  59.5 19.6 %collective-permute-done.10 = bf16[64,8192]{1,0:T(8,128)(2,1)} collective-permute-done((bf16[64,8192]{1,0:T(8,128)(2,1)}, bf16[64,8192]{1,0:T(8,128)(2,1)}, u32[]{:S(2)}, u32[]{:S(2)}) %collective-permute-start.10) | collective-permute-done | bytes 1048608 | tf_op jit(solution)/shard_map/ppermute | solution.py:13
  79.1 80.6 %collective-permute-done.11 = bf16[64,8192]{1,0:T(8,128)(2,1)} collective-permute-done((bf16[64,8192]{1,0:T(8,128)(2,1)}, bf16[64,8192]{1,0:T(8,128)(2,1)}, u32[]{:S(2)}, u32[]{:S(2)}) %collective-permute-start.11) | collective-permute-done | bytes 1048608 | tf_op jit(solution)/shard_map/ppermute | solution.py:13
  159.7 26.8 %collective-permute-done.12 = bf16[64,8192]{1,0:T(8,128)(2,1)} collective-permute-done((bf16[64,8192]{1,0:T(8,128)(2,1)}, bf16[64,8192]{1,0:T(8,128)(2,1)}, u32[]{:S(2)}, u32[]{:S(2)}) %collective-permute-start.12) | collective-permute-done | bytes 1048608 | tf_op jit(solution)/shard_map/ppermute | solution.py:13
  186.5 27.4 %collective-permute-done.13 = bf16[64,8192]{1,0:T(8,128)(2,1)} collective-permute-done((bf16[64,8192]{1,0:T(8,128)(2,1)}, bf16[64,8192]{1,0:T(8,128)(2,1)}, u32[]{:S(2)}, u32[]{:S(2)}) %collective-permute-start.13) | collective-permute-done | bytes 1048608 | tf_op jit(solution)/shard_map/ppermute | solution.py:13
  214.0 80.7 %collective-permute-done.14 = bf16[64,8192]{1,0:T(8,128)(2,1)} collective-permute-done((bf16[64,8192]{1,0:T(8,128)(2,1)}, bf16[64,8192]{1,0:T(8,128)(2,1)}, u32[]{:S(2)}, u32[]{:S(2)}) %collective-permute-start.14) | collective-permute-done | bytes 1048608 | tf_op jit(solution)/shard_map/ppermute | solution.py:13
  294.6 8.1 %fusion = f32[128,8192]{1,0:T(8,128)} fusion(bf16[8192,128,1]{0,1,2:T(8,128)(2,1)S(1)} %bitcast.91, bf16[1,64,8192]{2,1,0:T(8,128)(2,1)} %bitcast.33, bf16[1,64,8192]{2,1,0:T(8,128)(2,1)} %bitcast.32, bf16[1,64,8192]{2,1,0:T(8,128)(2,1)} %bitcast.31, bf16[1,64,8192]{2,1,0:T(8,128)(2,1)} %get-tuple-element.14, bf16[1,64,8192]{2,1,0:T(8,128)(2,1)} %bitcast.29, ...), kind=kOutput, calls=%fused_computation.1 | convolution fusion | flops 1087438848 | bytes 14682112 | tf_op jit(solution)/shard_map/njc,njd->cd/dot_general | solution.py:120
  305.9 1.9 select_bitcast_fusion.5
  307.8 1.2 collective-permute-start.1
  309.1 5.4 collective-permute-start.3
  314.4 9.1 %fusion.5 = f32[8192,128,1]{0,1,2:T(8,128)} fusion(bf16[128,8192,1]{1,0,2:T(8,128)(2,1)} %bitcast.92, bf16[1,64,8192]{2,1,0:T(8,128)(2,1)} %bitcast.33, bf16[1,64,8192]{2,1,0:T(8,128)(2,1)} %bitcast.32, bf16[1,64,8192]{2,1,0:T(8,128)(2,1)} %bitcast.31, bf16[1,64,8192]{2,1,0:T(8,128)(2,1)} %get-tuple-element.14, bf16[1,64,8192]{2,1,0:T(8,128)(2,1)} %bitcast.29, ...), kind=kOutput, calls=%fused_computation.16 | convolution fusion | flops 1086390272 | bytes 14682112 | tf_op jit(solution)/shard_map/njd,njc->dc/dot_general | solution.py:116
  323.6 1.6 copy-done.2
  325.2 0.2 select_bitcast_fusion.2
  325.4 1.0 collective-permute-start.6
  326.3 6.9 %collective-permute-start.7 = (bf16[64,8192]{1,0:T(8,128)(2,1)S(1)}, bf16[64,8192]{1,0:T(8,128)(2,1)S(1)}, u32[]{:S(2)}, u32[]{:S(2)}) collective-permute-start(bf16[64,8192]{1,0:T(8,128)(2,1)S(1)} %get-tuple-element.22), channel_id=1, source_target_pairs={{0,30},{1,31},{2,0},{3,1},{4,2},{5,3},{6,4},{7,5},{8,6},{9,7},{10,... | collective-permute-start | bytes 3145736 | tf_op jit(solution)/shard_map/ppermute | solution.py:13
  333.2 43.6 %collective-permute-done.1 = bf16[8192,64]{0,1:T(8,128)(2,1)S(1)} collective-permute-done((bf16[8192,64]{0,1:T(8,128)(2,1)}, bf16[8192,64]{0,1:T(8,128)(2,1)S(1)}, u32[]{:S(2)}, u32[]{:S(2)}) %collective-permute-start.1) | collective-permute-done | bytes 1048608 | tf_op jit(solution)/shard_map/ppermute | solution.py:13
  376.8 28.3 %collective-permute-done.3 = bf16[8192,64]{0,1:T(8,128)(2,1)} collective-permute-done((bf16[8192,64]{0,1:T(8,128)(2,1)}, bf16[8192,64]{0,1:T(8,128)(2,1)}, u32[]{:S(2)}, u32[]{:S(2)}) %collective-permute-start.3) | collective-permute-done | bytes 1048608 | tf_op jit(solution)/shard_map/ppermute | solution.py:13
  405.1 38.4 %collective-permute-done.5 = bf16[8192,64]{0,1:T(8,128)(2,1)} collective-permute-done((bf16[8192,64]{0,1:T(8,128)(2,1)}, bf16[8192,64]{0,1:T(8,128)(2,1)}, u32[]{:S(2)}, u32[]{:S(2)}) %collective-permute-start.5) | collective-permute-done | bytes 1048608 | tf_op jit(solution)/shard_map/ppermute | solution.py:13
  443.6 1.8 fusion.15
  445.4 66.3 %collective-permute-done.6 = bf16[64,8192]{1,0:T(8,128)(2,1)S(1)} collective-permute-done((bf16[64,8192]{1,0:T(8,128)(2,1)S(1)}, bf16[64,8192]{1,0:T(8,128)(2,1)S(1)}, u32[]{:S(2)}, u32[]{:S(2)}) %collective-permute-start.6) | collective-permute-done | bytes 1048608 | tf_op jit(solution)/shard_map/ppermute | solution.py:13
  511.6 28.2 %collective-permute-done.7 = bf16[64,8192]{1,0:T(8,128)(2,1)S(1)} collective-permute-done((bf16[64,8192]{1,0:T(8,128)(2,1)S(1)}, bf16[64,8192]{1,0:T(8,128)(2,1)S(1)}, u32[]{:S(2)}, u32[]{:S(2)}) %collective-permute-start.7) | collective-permute-done | bytes 1048608 | tf_op jit(solution)/shard_map/ppermute | solution.py:13
  539.9 38.1 %collective-permute-done.8 = bf16[64,8192]{1,0:T(8,128)(2,1)S(1)} collective-permute-done((bf16[64,8192]{1,0:T(8,128)(2,1)S(1)}, bf16[64,8192]{1,0:T(8,128)(2,1)S(1)}, u32[]{:S(2)}, u32[]{:S(2)}) %collective-permute-start.8) | collective-permute-done | bytes 1048608 | tf_op jit(solution)/shard_map/ppermute | solution.py:13
  577.9 1.2 fusion.13
  579.2 3.9 convolution_convert_fusion.1
  583.1 4.0 fusion.1
  587.0 3.6 convolution_convert_fusion
  590.6 3.7 fusion.2
  594.3 2.9 pad_maximum_fusion.3
  597.2 1.5 pad_maximum_fusion.2
  598.7 1.8 convert_element_type.63
  600.4 1.8 convert_element_type.61
  (33 shorter events, 0.3 us)
Async XLA Ops:
  7.2 591.5 %reduce-scatter.5.cloned.1.call-start = ((), (), s32[]{:S(2)}) async-start(), calls=%async_computation.3 | async-start | bytes 4718592 | tf_op jit(solution)/shard_map/reduce_scatter | solution.py:126
  11.7 23.0 %collective-permute-start = (s32[1]{0:T(128)}, s32[1]{0:T(128)}, u32[]{:S(2)}, u32[]{:S(2)}) collective-permute-start(s32[1]{0:T(128)} %bitcast.4), channel_id=1, source_target_pairs={{0,3},{1,4},{2,5},{3,6},{4,7},{5,8},{6,9},{7,10},{8,11},{9,12},{10... | collective-permute-start | bytes 20 | tf_op jit(solution)/shard_map/ppermute | solution.py:13
  19.8 18.7 %collective-permute-start.2 = (s32[1]{0:T(128)}, s32[1]{0:T(128)}, u32[]{:S(2)}, u32[]{:S(2)}) collective-permute-start(s32[1]{0:T(128)} %bitcast.9), channel_id=1, source_target_pairs={{0,2},{1,3},{2,4},{3,5},{4,6},{5,7},{6,8},{7,9},{8,10},{9,11},{10,... | collective-permute-start | bytes 20 | tf_op jit(solution)/shard_map/ppermute | solution.py:13
  24.4 14.8 %collective-permute-start.4 = (s32[1]{0:T(128)}, s32[1]{0:T(128)}, u32[]{:S(2)}, u32[]{:S(2)}) collective-permute-start(s32[1]{0:T(128)} %bitcast.14), channel_id=1, source_target_pairs={{0,1},{1,2},{2,3},{3,4},{4,5},{5,6},{6,7},{7,8},{8,9},{9,10},{10,1... | collective-permute-start | bytes 20 | tf_op jit(solution)/shard_map/ppermute | solution.py:13
  26.5 6.1 copy-start.4
  29.8 264.8 %copy-start.8 = (bf16[1,64,8192]{2,1,0:T(8,128)(2,1)}, bf16[1,64,8192]{2,1,0:T(8,128)(2,1)S(1)}, u32[]{:S(2)}) copy-start(bf16[1,64,8192]{2,1,0:T(8,128)(2,1)S(1)} %get-tuple-element.10) | copy-start | bytes 3145732
  29.8 21.8 %collective-permute-start.9 = (bf16[64,8192]{1,0:T(8,128)(2,1)S(1)}, bf16[64,8192]{1,0:T(8,128)(2,1)S(1)}, u32[]{:S(2)}, u32[]{:S(2)}) collective-permute-start(bf16[64,8192]{1,0:T(8,128)(2,1)S(1)} %get-tuple-element.11), channel_id=1, source_target_pairs={{0,1},{1,2},{2,3},{3,4},{4,5},{5,6},{6,7},{7,8},{8,9},{9,10},{10,1... | collective-permute-start | bytes 3145736 | tf_op jit(solution)/shard_map/ppermute | solution.py:13
  30.1 264.5 %copy-start = (bf16[2,8192,64]{1,2,0:T(8,128)(2,1)S(1)}, bf16[2,8192,64]{1,2,0:T(8,128)(2,1)}, u32[]{:S(2)}) copy-start(bf16[2,8192,64]{1,2,0:T(8,128)(2,1)} %param.7) | copy-start | bytes 6291460
  30.1 49.0 %collective-permute-start.10 = (bf16[64,8192]{1,0:T(8,128)(2,1)}, bf16[64,8192]{1,0:T(8,128)(2,1)}, u32[]{:S(2)}, u32[]{:S(2)}) collective-permute-start(bf16[64,8192]{1,0:T(8,128)(2,1)} %get-tuple-element.12), channel_id=1, source_target_pairs={{0,2},{1,3},{2,4},{3,5},{4,6},{5,7},{6,8},{7,9},{8,10},{9,11},{10,... | collective-permute-start | bytes 3145736 | tf_op jit(solution)/shard_map/ppermute | solution.py:13
  34.7 125.0 %collective-permute-start.11 = (bf16[64,8192]{1,0:T(8,128)(2,1)}, bf16[64,8192]{1,0:T(8,128)(2,1)}, u32[]{:S(2)}, u32[]{:S(2)}) collective-permute-start(bf16[64,8192]{1,0:T(8,128)(2,1)} %get-tuple-element.13), channel_id=1, source_target_pairs={{0,3},{1,4},{2,5},{3,6},{4,7},{5,8},{6,9},{7,10},{8,11},{9,12},{10... | collective-permute-start | bytes 3145736 | tf_op jit(solution)/shard_map/ppermute | solution.py:13
  38.5 148.0 %collective-permute-start.12 = (bf16[64,8192]{1,0:T(8,128)(2,1)}, bf16[64,8192]{1,0:T(8,128)(2,1)}, u32[]{:S(2)}, u32[]{:S(2)}) collective-permute-start(bf16[64,8192]{1,0:T(8,128)(2,1)} %get-tuple-element.15), channel_id=1, source_target_pairs={{0,1},{1,2},{2,3},{3,4},{4,5},{5,6},{6,7},{7,8},{8,9},{9,10},{10,1... | collective-permute-start | bytes 3145736 | tf_op jit(solution)/shard_map/ppermute | solution.py:13
  39.2 174.7 %collective-permute-start.13 = (bf16[64,8192]{1,0:T(8,128)(2,1)}, bf16[64,8192]{1,0:T(8,128)(2,1)}, u32[]{:S(2)}, u32[]{:S(2)}) collective-permute-start(bf16[64,8192]{1,0:T(8,128)(2,1)} %get-tuple-element.16), channel_id=1, source_target_pairs={{0,2},{1,3},{2,4},{3,5},{4,6},{5,7},{6,8},{7,9},{8,10},{9,11},{10,... | collective-permute-start | bytes 3145736 | tf_op jit(solution)/shard_map/ppermute | solution.py:13
  51.6 1.0 copy-start.9
  52.6 242.1 %collective-permute-start.14 = (bf16[64,8192]{1,0:T(8,128)(2,1)}, bf16[64,8192]{1,0:T(8,128)(2,1)}, u32[]{:S(2)}, u32[]{:S(2)}) collective-permute-start(bf16[64,8192]{1,0:T(8,128)(2,1)} %get-tuple-element.17), channel_id=1, source_target_pairs={{0,3},{1,4},{2,5},{3,6},{4,7},{5,8},{6,9},{7,10},{8,11},{9,12},{10... | collective-permute-start | bytes 3145736 | tf_op jit(solution)/shard_map/ppermute | solution.py:13
  302.8 297.7 %reduce-scatter.3.cloned.1.call-start = ((), (), s32[]{:S(2)}) async-start(), calls=%async_computation.2 | async-start | bytes 4718592 | tf_op jit(solution)/shard_map/reduce_scatter | solution.py:125
  307.8 69.0 %collective-permute-start.1 = (bf16[8192,64]{0,1:T(8,128)(2,1)}, bf16[8192,64]{0,1:T(8,128)(2,1)S(1)}, u32[]{:S(2)}, u32[]{:S(2)}) collective-permute-start(bf16[8192,64]{0,1:T(8,128)(2,1)} %get-tuple-element.20), channel_id=1, source_target_pairs={{0,29},{1,30},{2,31},{3,0},{4,1},{5,2},{6,3},{7,4},{8,5},{9,6},{10... | collective-permute-start | bytes 3145736 | tf_op jit(solution)/shard_map/ppermute | solution.py:13
  309.1 96.1 %collective-permute-start.3 = (bf16[8192,64]{0,1:T(8,128)(2,1)}, bf16[8192,64]{0,1:T(8,128)(2,1)}, u32[]{:S(2)}, u32[]{:S(2)}) collective-permute-start(bf16[8192,64]{0,1:T(8,128)(2,1)} %get-tuple-element.19), channel_id=1, source_target_pairs={{0,30},{1,31},{2,0},{3,1},{4,2},{5,3},{6,4},{7,5},{8,6},{9,7},{10,... | collective-permute-start | bytes 3145736 | tf_op jit(solution)/shard_map/ppermute | solution.py:13
  314.4 129.1 %collective-permute-start.5 = (bf16[8192,64]{0,1:T(8,128)(2,1)}, bf16[8192,64]{0,1:T(8,128)(2,1)}, u32[]{:S(2)}, u32[]{:S(2)}) collective-permute-start(bf16[8192,64]{0,1:T(8,128)(2,1)} %get-tuple-element.18), channel_id=1, source_target_pairs={{0,31},{1,0},{2,1},{3,2},{4,3},{5,4},{6,5},{7,6},{8,7},{9,8},{10,9... | collective-permute-start | bytes 3145736 | tf_op jit(solution)/shard_map/ppermute | solution.py:13
  323.5 1.6 copy-start.2
  325.2 118.4 %copy-start.1 = (bf16[2,8192,64]{1,2,0:T(8,128)(2,1)S(1)}, bf16[2,8192,64]{1,2,0:T(8,128)(2,1)}, u32[]{:S(2)}) copy-start(bf16[2,8192,64]{1,2,0:T(8,128)(2,1)} %param.7) | copy-start | bytes 6291460
  325.4 186.3 %collective-permute-start.6 = (bf16[64,8192]{1,0:T(8,128)(2,1)S(1)}, bf16[64,8192]{1,0:T(8,128)(2,1)S(1)}, u32[]{:S(2)}, u32[]{:S(2)}) collective-permute-start(bf16[64,8192]{1,0:T(8,128)(2,1)S(1)} %get-tuple-element.23), channel_id=1, source_target_pairs={{0,29},{1,30},{2,31},{3,0},{4,1},{5,2},{6,3},{7,4},{8,5},{9,6},{10... | collective-permute-start | bytes 3145736 | tf_op jit(solution)/shard_map/ppermute | solution.py:13
  326.3 213.5 %collective-permute-start.7 = (bf16[64,8192]{1,0:T(8,128)(2,1)S(1)}, bf16[64,8192]{1,0:T(8,128)(2,1)S(1)}, u32[]{:S(2)}, u32[]{:S(2)}) collective-permute-start(bf16[64,8192]{1,0:T(8,128)(2,1)S(1)} %get-tuple-element.22), channel_id=1, source_target_pairs={{0,30},{1,31},{2,0},{3,1},{4,2},{5,3},{6,4},{7,5},{8,6},{9,7},{10,... | collective-permute-start | bytes 3145736 | tf_op jit(solution)/shard_map/ppermute | solution.py:13
  376.8 201.1 %copy-start.3 = (bf16[2,64,8192]{2,1,0:T(8,128)(2,1)S(1)}, bf16[2,64,8192]{2,1,0:T(8,128)(2,1)}, u32[]{:S(2)}) copy-start(bf16[2,64,8192]{2,1,0:T(8,128)(2,1)} %param.8) | copy-start | bytes 6291460
  376.8 201.1 %collective-permute-start.8 = (bf16[64,8192]{1,0:T(8,128)(2,1)S(1)}, bf16[64,8192]{1,0:T(8,128)(2,1)S(1)}, u32[]{:S(2)}, u32[]{:S(2)}) collective-permute-start(bf16[64,8192]{1,0:T(8,128)(2,1)S(1)} %get-tuple-element.21), channel_id=1, source_target_pairs={{0,31},{1,0},{2,1},{3,2},{4,3},{5,4},{6,5},{7,6},{8,7},{9,8},{10,9... | collective-permute-start | bytes 3145736 | tf_op jit(solution)/shard_map/ppermute | solution.py:13
  590.6 3.7 copy-start.6
  594.3 2.9 copy-start.5
  594.3 2.9 copy-start.7
Sparse Core Ops, SparseCore 0:
  302.9 48.1 reduce-scatter.4
  353.7 40.2 reduce-scatter.2

commit v2 on v1

v2 whole, which is shorter than its diff:
```python
import jax
import jax.numpy as jnp
from jax import lax
from jax.sharding import PartitionSpec as P


adapter_scale = 2.0


def shifted(value, axis, steps):
    count = lax.axis_size(axis)
    pairs = [(source, (source + steps) % count) for source in range(count)]
    return lax.ppermute(value, axis, pairs)


def pick(selector, choices, fallback):
    out = fallback
    for index, choice in enumerate(choices):
        out = jnp.where(selector == index, choice, out)
    return out


def on_device(tokens, grad_out, down_panels, up_panels, seg_adapter):
    groups = lax.axis_size("adapter")
    held_count, feat_width, rank_size = down_panels.shape
    segs_here = seg_adapter.shape[0]
    seg_rows = tokens.shape[0] // segs_here
    reach_count = 2 * segs_here
    position = lax.axis_index("adapter")
    owners_of = seg_adapter // held_count
    local_index = seg_adapter - owners_of * held_count
    distance = jnp.mod(owners_of - position, groups)

    token_blocks = tokens.reshape(segs_here, seg_rows, feat_width)
    grad_blocks = grad_out.reshape(segs_here, seg_rows, feat_width)

    def slot_of(blocks, slot_index):
        out = jnp.zeros_like(blocks[0])
        for seg in range(segs_here):
            out = jnp.where(distance[seg] == slot_index, blocks[seg], out)
        return out

    def selector_of(slot_index):
        sel = jnp.int32(-1)
        for seg in range(segs_here):
            sel = jnp.where(distance[seg] == slot_index, local_index[seg], sel)
        return sel.reshape(1)

    sel_list = [selector_of(k) for k in range(reach_count)]
    arrived_sel = [sel_list[0]]
    for k in range(1, reach_count):
        arrived_sel.append(shifted(sel_list[k], "adapter", k))

    both_blocks = jnp.stack([token_blocks, grad_blocks], axis=1)
    pay_list = [slot_of(both_blocks, k) for k in range(reach_count)]
    for k in range(1, reach_count):
        pay_list[k] = shifted(pay_list[k], "adapter", k)

    panels_joined = jnp.stack([jnp.transpose(down_panels, (0, 2, 1)), up_panels], axis=1)
    panel_list = [panels_joined[i] for i in range(held_count)]
    wt_back = [None] * reach_count
    for k in range(1, reach_count):
        wt_back[k] = shifted(pick(arrived_sel[k][0], panel_list, panel_list[0]), "adapter", -k)

    outs = []
    backs = []
    contract_last = (((1,), (1,)), ((), ()))
    for seg in range(segs_here):
        seg_panels = pick(local_index[seg], panel_list, panel_list[0])
        for k in range(1, reach_count):
            seg_panels = jnp.where(distance[seg] == k, wt_back[k], seg_panels)
        seg_down_t = seg_panels[0]
        seg_up = seg_panels[1]
        hidden = lax.dot_general(
            token_blocks[seg], seg_down_t, contract_last, preferred_element_type=jnp.float32
        ).astype(jnp.bfloat16)
        outs.append(
            (adapter_scale * jnp.dot(hidden, seg_up, preferred_element_type=jnp.float32)).astype(
                jnp.bfloat16
            )
        )
        hidden_grad = (
            adapter_scale
            * lax.dot_general(
                grad_blocks[seg], seg_up, contract_last, preferred_element_type=jnp.float32
            )
        ).astype(jnp.bfloat16)
        backs.append(
            jnp.dot(hidden_grad, seg_down_t, preferred_element_type=jnp.float32).astype(jnp.bfloat16)
        )
    adapter_out = jnp.concatenate(outs, axis=0)
    grad_tokens = jnp.concatenate(backs, axis=0)

    arrived = jnp.stack(pay_list)
    arrived_rows = arrived[:, 0]
    arrived_grads = arrived[:, 1]
    arrived_select = jnp.concatenate(arrived_sel).astype(jnp.float32)
    picks = (
        arrived_select[:, None] == jnp.arange(held_count, dtype=jnp.float32)[None, :]
    ).astype(jnp.float32)
    masking = jnp.repeat(picks, rank_size, axis=1)[:, None, :]
    down_cat = jnp.transpose(down_panels, (1, 0, 2)).reshape(feat_width, held_count * rank_size)
    up_weight_joined = up_panels.reshape(held_count * rank_size, feat_width)
    hidden_state = (
        jnp.einsum("njd,dc->njc", arrived_rows, down_cat, preferred_element_type=jnp.float32)
        * masking
    ).astype(jnp.bfloat16)
    hidden_gradient = adapter_scale * jnp.einsum(
        "njd,cd->njc", arrived_grads, up_weight_joined, preferred_element_type=jnp.float32
    )
    hidden_gradient = (hidden_gradient * masking).astype(jnp.bfloat16)
    down_sum = jnp.einsum(
        "njd,njc->dc", arrived_rows, hidden_gradient, preferred_element_type=jnp.float32
    )
    up_sum_t = adapter_scale * jnp.einsum(
        "njd,njc->dc", arrived_grads, hidden_state, preferred_element_type=jnp.float32
    )
    joined = jnp.concatenate([down_sum, up_sum_t], axis=1)
    summed = lax.psum_scatter(joined, "dp", scatter_dimension=0, tiled=True)
    width = held_count * rank_size
    part_rows = summed.shape[0]
    grad_down = jnp.transpose(summed[:, :width].reshape(part_rows, held_count, rank_size), (1, 0, 2))
    grad_up = jnp.transpose(summed[:, width:].reshape(part_rows, held_count, rank_size), (1, 2, 0))
    return (adapter_out, grad_tokens, grad_down.astype(jnp.bfloat16), grad_up.astype(jnp.bfloat16))


def solution(mesh):
    placed = (
        P(("dp", "adapter"), None),
        P(("dp", "adapter"), None),
        P("adapter", None, None),
        P("adapter", None, None),
        P(("dp", "adapter")),
    )
    return jax.shard_map(
        on_device,
        mesh=mesh,
        in_specs=placed,
        out_specs=(
            P(("dp", "adapter"), None),
            P(("dp", "adapter"), None),
            P("adapter", "dp", None),
            P("adapter", None, "dp"),
        ),
        check_vma=False,
    )
```

time: 616 us -> 653 us (1.060)
  starting transfers between devices: 33.6 us -> 280 us
  waiting for transfers between devices: 490 us -> 270 us
  other arithmetic: 21.2 us -> 39.9 us
    ppermute x15 -> x9, starting transfers between devices: 33.5 us -> 280 us  [shifted(): return lax.ppermute(value, axis, pairs)]
    ppermute x15 -> x9, waiting for transfers between devices: 490 us -> 270 us  [shifted(): return lax.ppermute(value, axis, pairs)]
    select_n x2 -> x3, other arithmetic: 3.06 us -> 10.6 us  [the longest x2 5.59 us: slot_of(): out = jnp.where(distance[seg] == slot_index, blocks[seg], out)]
  transfers between devices with their start and end apart: 17 -> 10, of which waited for: 12 -> 4; matrix products, arithmetic and copies ran while one was open for 7% -> 5% of each run, Pallas kernels for 0% -> 0%
where the time goes in v2:
time: 653 us; the launch traced here: 651 us
  starting transfers between devices  280 us (43%)
  waiting for transfers between devices  270 us (41%)
  other arithmetic  39.9 us (6%)
  matrix products  32.3 us (5%)
  between operations  27.5 us (4%)
    ppermute x9, starting transfers between devices, shifted(): return lax.ppermute(value, axis, pairs)  280 us
    ppermute x9, waiting for transfers between devices, shifted(): return lax.ppermute(value, axis, pairs)  270 us
  transfers between devices with their start and end apart: 10, of which 4 were waited for; matrix products, arithmetic and copies ran while one was open for 5% of the time, Pallas kernels for 0%

profile of v2, /device:TPU:71, one launch (start us, length us, event | category | flops | bytes accessed | tf_op | source)
XLA Modules:
  0.0 651.0 jit_solution(14294938483655309655)
XLA Ops:
  7.2 0.0 reduce-scatter.2.cloned.1.call-start
  7.2 0.7 multiply_subtract_fusion
  7.9 0.6 fusion.42
  13.7 3.4 select_bitcast_fusion.3
  17.0 2.2 select_bitcast_fusion.2
  19.3 1.6 collective-permute-start.6
  20.9 3.3 collective-permute-start.7
  24.2 0.9 collective-permute-start.8
  25.1 0.6 fusion.41
  27.0 261.5 %collective-permute-start = (s32[1]{0:T(128)}, s32[1]{0:T(128)}, u32[]{:S(2)}, u32[]{:S(2)}) collective-permute-start(s32[1]{0:T(128)} %bitcast.4), channel_id=1, source_target_pairs={{0,3},{1,4},{2,5},{3,6},{4,7},{5,8},{6,9},{7,10},{8,11},{9,12},{10... | collective-permute-start | bytes 20 | tf_op jit(solution)/shard_map/ppermute | solution.py:13
  289.8 1.1 collective-permute-start.2
  293.5 0.0 collective-permute-done
  293.5 5.0 collective-permute-start.4
  298.5 0.0 collective-permute-done.2
  298.5 1.5 collective-permute-done.4
  300.0 2.0 add_convert_fusion
  302.0 0.1 fusion.34
  302.1 0.1 broadcast_in_dim.2
  302.1 0.1 mul.52
  302.2 0.0 collective-permute-done.6
  302.2 0.0 collective-permute-done.7
  302.2 0.0 collective-permute-done.8
  302.2 0.0 copy-start.2
  302.3 7.3 %pad_maximum_fusion = bf16[4,2,64,8192]{3,2,0,1:T(8,128)(2,1)} fusion(bf16[1,2,64,8192]{3,2,0,1:T(8,128)(2,1)} %bitcast.43, bf16[1,2,64,8192]{3,2,0,1:T(8,128)(2,1)} %bitcast.41, bf16[1,2,64,8192]{3,2,0,1:T(8,128)(2,1)} %bitcast.38, bf16[1,2,64,8192]{3,2,0,1:T(8,128)(2,1)} %get-tuple-element.4), kind=kLoop, calls=%fused_computation.9 | loop fusion | flops 12582912 | bytes 16777216 | tf_op jit(solution)/shard_map/stack | solution.py:94
  309.5 0.0 copy-done.2
  309.6 8.4 %fusion = f32[8192,128]{0,1:T(8,128)} fusion(bf16[4,2,64,8192]{3,2,0,1:T(8,128)(2,1)} %pad_maximum_fusion, bf16[8192,128,1]{0,1,2:T(8,128)(2,1)S(1)} %bitcast.150, f32[4,128]{1,0:T(4,128)S(1)} %mul.52), kind=kOutput, calls=%fused_computation.2 | convolution fusion | flops 1074855936 | bytes 14682112 | tf_op jit(solution)/shard_map/njd,njc->dc/dot_general | solution.py:115
  318.0 9.0 %convolution_bitcast_fusion.1 = f32[8192,128]{0,1:T(8,128)} fusion(bf16[4,2,64,8192]{3,2,0,1:T(8,128)(2,1)} %pad_maximum_fusion, bf16[128,8192,1]{1,0,2:T(8,128)(2,1)} %bitcast.153, f32[4,128]{1,0:T(4,128)S(1)} %broadcast_multiply_fusion), kind=kOutput, calls=%fused_computation.1 | convolution fusion | flops 1073807360 | bytes 14682112 | tf_op jit(solution)/shard_map/njd,njc->dc/dot_general | solution.py:112
  327.0 7.6 %pad_maximum_fusion.1 = f32[8192,256]{0,1:T(8,128)} fusion(f32[8192,128]{0,1:T(8,128)} %fusion, f32[8192,128]{0,1:T(8,128)} %convolution_bitcast_fusion.1), kind=kLoop, calls=%fused_computation.10 | loop fusion | flops 2097152 | bytes 16777216 | tf_op jit(solution)/shard_map/concatenate | solution.py:118
  334.6 0.0 reduce-scatter.2.cloned.1.call-update
  336.5 3.3 fusion.9
  339.9 2.7 fusion.8
  342.6 0.0 copy-done
  342.6 1.9 collective-permute-start.1
  344.5 1.0 collective-permute-start.3
  345.5 3.1 collective-permute-start.5
  349.9 128.4 %collective-permute-done.1 = bf16[2,64,8192]{2,1,0:T(8,128)(2,1)} collective-permute-done((bf16[2,64,8192]{2,1,0:T(8,128)(2,1)}, bf16[2,64,8192]{2,1,0:T(8,128)(2,1)}, u32[]{:S(2)}, u32[]{:S(2)}) %collective-permute-start.1) | collective-permute-done | bytes 2097184 | tf_op jit(solution)/shard_map/ppermute | solution.py:13
  478.3 74.5 %collective-permute-done.3 = bf16[2,64,8192]{2,1,0:T(8,128)(2,1)} collective-permute-done((bf16[2,64,8192]{2,1,0:T(8,128)(2,1)}, bf16[2,64,8192]{2,1,0:T(8,128)(2,1)}, u32[]{:S(2)}, u32[]{:S(2)}) %collective-permute-start.3) | collective-permute-done | bytes 2097184 | tf_op jit(solution)/shard_map/ppermute | solution.py:13
  552.8 65.1 %collective-permute-done.5 = bf16[2,64,8192]{2,1,0:T(8,128)(2,1)} collective-permute-done((bf16[2,64,8192]{2,1,0:T(8,128)(2,1)}, bf16[2,64,8192]{2,1,0:T(8,128)(2,1)}, u32[]{:S(2)}, u32[]{:S(2)}) %collective-permute-start.5) | collective-permute-done | bytes 2097184 | tf_op jit(solution)/shard_map/ppermute | solution.py:13
  617.9 5.0 fusion.13
  622.9 3.2 convolution_convert_fusion.1
  626.1 0.0 copy-start.1
  626.2 4.4 fusion.1
  630.5 0.0 copy-done.1
  630.5 3.6 convolution_convert_fusion
  634.1 3.7 fusion.2
  637.8 4.3 pad_maximum_fusion.4
  642.1 1.3 convert.4
  643.4 0.8 fusion.40
  (4 shorter events, 0.0 us)
Async XLA Ops:
  7.2 634.9 %reduce-scatter.2.cloned.1.call-start = ((), (), s32[]{:S(2)}) async-start(), calls=%async_computation.1 | async-start | bytes 9437184 | tf_op jit(solution)/shard_map/reduce_scatter | solution.py:119
  19.3 283.0 %collective-permute-start.6 = (bf16[2,64,8192]{2,1,0:T(8,128)(2,1)}, bf16[2,64,8192]{2,1,0:T(8,128)(2,1)}, u32[]{:S(2)}, u32[]{:S(2)}) collective-permute-start(bf16[2,64,8192]{2,1,0:T(8,128)(2,1)} %get-tuple-element.14), channel_id=1, source_target_pairs={{0,1},{1,2},{2,3},{3,4},{4,5},{5,6},{6,7},{7,8},{8,9},{9,10},{10,1... | collective-permute-start | bytes 6291464 | tf_op jit(solution)/shard_map/ppermute | solution.py:13
  20.9 281.3 %collective-permute-start.7 = (bf16[2,64,8192]{2,1,0:T(8,128)(2,1)}, bf16[2,64,8192]{2,1,0:T(8,128)(2,1)}, u32[]{:S(2)}, u32[]{:S(2)}) collective-permute-start(bf16[2,64,8192]{2,1,0:T(8,128)(2,1)} %get-tuple-element.15), channel_id=1, source_target_pairs={{0,2},{1,3},{2,4},{3,5},{4,6},{5,7},{6,8},{7,9},{8,10},{9,11},{10,... | collective-permute-start | bytes 6291464 | tf_op jit(solution)/shard_map/ppermute | solution.py:13
  24.2 278.0 %collective-permute-start.8 = (bf16[2,64,8192]{2,1,0:T(8,128)(2,1)S(1)}, bf16[2,64,8192]{2,1,0:T(8,128)(2,1)}, u32[]{:S(2)}, u32[]{:S(2)}) collective-permute-start(bf16[2,64,8192]{2,1,0:T(8,128)(2,1)S(1)} %get-tuple-element.16), channel_id=1, source_target_pairs={{0,3},{1,4},{2,5},{3,6},{4,7},{5,8},{6,9},{7,10},{8,11},{9,12},{10... | collective-permute-start | bytes 6291464 | tf_op jit(solution)/shard_map/ppermute | solution.py:13
  27.0 266.5 %collective-permute-start = (s32[1]{0:T(128)}, s32[1]{0:T(128)}, u32[]{:S(2)}, u32[]{:S(2)}) collective-permute-start(s32[1]{0:T(128)} %bitcast.4), channel_id=1, source_target_pairs={{0,3},{1,4},{2,5},{3,6},{4,7},{5,8},{6,9},{7,10},{8,11},{9,12},{10... | collective-permute-start | bytes 20 | tf_op jit(solution)/shard_map/ppermute | solution.py:13
  289.8 8.7 %collective-permute-start.2 = (s32[1]{0:T(128)}, s32[1]{0:T(128)}, u32[]{:S(2)}, u32[]{:S(2)}) collective-permute-start(s32[1]{0:T(128)} %bitcast.13), channel_id=1, source_target_pairs={{0,2},{1,3},{2,4},{3,5},{4,6},{5,7},{6,8},{7,9},{8,10},{9,11},{10,... | collective-permute-start | bytes 20 | tf_op jit(solution)/shard_map/ppermute | solution.py:13
  293.5 6.5 %collective-permute-start.4 = (s32[1]{0:T(128)}, s32[1]{0:T(128)}, u32[]{:S(2)}, u32[]{:S(2)}) collective-permute-start(s32[1]{0:T(128)} %bitcast.19), channel_id=1, source_target_pairs={{0,1},{1,2},{2,3},{3,4},{4,5},{5,6},{6,7},{7,8},{8,9},{9,10},{10,1... | collective-permute-start | bytes 20 | tf_op jit(solution)/shard_map/ppermute | solution.py:13
  302.2 7.3 %copy-start.2 = (bf16[2,8192,64]{1,2,0:T(8,128)(2,1)S(1)}, bf16[2,8192,64]{1,2,0:T(8,128)(2,1)}, u32[]{:S(2)}) copy-start(bf16[2,8192,64]{1,2,0:T(8,128)(2,1)} %param.7) | copy-start | bytes 6291460
  339.9 2.7 copy-start
  342.6 135.7 %collective-permute-start.1 = (bf16[2,64,8192]{2,1,0:T(8,128)(2,1)}, bf16[2,64,8192]{2,1,0:T(8,128)(2,1)}, u32[]{:S(2)}, u32[]{:S(2)}) collective-permute-start(bf16[2,64,8192]{2,1,0:T(8,128)(2,1)} %get-tuple-element.18), channel_id=1, source_target_pairs={{0,29},{1,30},{2,31},{3,0},{4,1},{5,2},{6,3},{7,4},{8,5},{9,6},{10... | collective-permute-start | bytes 6291464 | tf_op jit(solution)/shard_map/ppermute | solution.py:13
  344.5 208.2 %collective-permute-start.3 = (bf16[2,64,8192]{2,1,0:T(8,128)(2,1)}, bf16[2,64,8192]{2,1,0:T(8,128)(2,1)}, u32[]{:S(2)}, u32[]{:S(2)}) collective-permute-start(bf16[2,64,8192]{2,1,0:T(8,128)(2,1)} %get-tuple-element.17), channel_id=1, source_target_pairs={{0,30},{1,31},{2,0},{3,1},{4,2},{5,3},{6,4},{7,5},{8,6},{9,7},{10,... | collective-permute-start | bytes 6291464 | tf_op jit(solution)/shard_map/ppermute | solution.py:13
  345.5 272.3 %collective-permute-start.5 = (bf16[2,64,8192]{2,1,0:T(8,128)(2,1)}, bf16[2,64,8192]{2,1,0:T(8,128)(2,1)}, u32[]{:S(2)}, u32[]{:S(2)}) collective-permute-start(bf16[2,64,8192]{2,1,0:T(8,128)(2,1)} %get-tuple-element.7), channel_id=1, source_target_pairs={{0,31},{1,0},{2,1},{3,2},{4,3},{5,4},{6,5},{7,6},{8,7},{9,8},{10,9... | collective-permute-start | bytes 6291464 | tf_op jit(solution)/shard_map/ppermute | solution.py:13
  626.1 4.4 copy-start.1
Sparse Core Ops, SparseCore 0:
  334.8 57.7 reduce-scatter.1

commit v3 on v2

--- a/solution.py
+++ b/solution.py
@@ -109,19 +109,24 @@
         "njd,cd->njc", arrived_grads, up_weight_joined, preferred_element_type=jnp.float32
     )
     hidden_gradient = (hidden_gradient * masking).astype(jnp.bfloat16)
-    down_sum = jnp.einsum(
-        "njd,njc->dc", arrived_rows, hidden_gradient, preferred_element_type=jnp.float32
+    zero_half = jnp.zeros_like(hidden_gradient)
+    doubled_hidden = (adapter_scale * hidden_state.astype(jnp.float32)).astype(jnp.bfloat16)
+    blocks_right = jnp.stack(
+        [
+            jnp.concatenate([hidden_gradient, zero_half], axis=-1),
+            jnp.concatenate([zero_half, doubled_hidden], axis=-1),
+        ],
+        axis=1,
     )
-    up_sum_t = adapter_scale * jnp.einsum(
-        "njd,njc->dc", arrived_grads, hidden_state, preferred_element_type=jnp.float32
-    )
-    joined = jnp.concatenate([down_sum, up_sum_t], axis=1)
+    joined = jnp.einsum(
+        "nwjd,nwjc->dc", arrived, blocks_right, preferred_element_type=jnp.float32
+    ).astype(jnp.bfloat16)
     summed = lax.psum_scatter(joined, "dp", scatter_dimension=0, tiled=True)
     width = held_count * rank_size
     part_rows = summed.shape[0]
     grad_down = jnp.transpose(summed[:, :width].reshape(part_rows, held_count, rank_size), (1, 0, 2))
     grad_up = jnp.transpose(summed[:, width:].reshape(part_rows, held_count, rank_size), (1, 2, 0))
-    return (adapter_out, grad_tokens, grad_down.astype(jnp.bfloat16), grad_up.astype(jnp.bfloat16))
+    return (adapter_out, grad_tokens, grad_down, grad_up)
 
 
 def solution(mesh):

time: 653 us -> 635 us (0.972)
  matrix products: 32.3 us -> 21.7 us
  other arithmetic: 39.9 us -> 30.1 us
    dot_general x2 -> x3, matrix products: 17.4 us -> 6.86 us  [the longest x1 4.37 us: on_device(): jnp.einsum('nwjd,nwjc->dc', arrived, blocks_right, preferred_element_type...]
    concatenate x1 -> x0, other arithmetic: 7.63 us -> none  [on_device(): joined = jnp.concatenate([down_sum, up_sum_t], axis=1)]
where the time goes in v3:
time: 635 us; the launch traced here: 633 us
  starting transfers between devices  279 us (44%)
  waiting for transfers between devices  270 us (43%)
  other arithmetic  30.1 us (5%)
  between operations  27.8 us (4%)
  matrix products  21.7 us (3%)
    ppermute x9, starting transfers between devices, shifted(): return lax.ppermute(value, axis, pairs)  279 us
    ppermute x9, waiting for transfers between devices, shifted(): return lax.ppermute(value, axis, pairs)  270 us
  transfers between devices with their start and end apart: 10, of which 4 were waited for; matrix products, arithmetic and copies ran while one was open for 5% of the time, Pallas kernels for 0%

profile of v3, /device:TPU:71, one launch (start us, length us, event | category | flops | bytes accessed | tf_op | source)
XLA Modules:
  0.0 633.1 jit_solution(5549311723808022916)
XLA Ops:
  7.2 0.0 reduce-scatter.2.cloned.1.call-start
  7.2 0.7 multiply_subtract_fusion
  7.9 0.6 fusion.45
  13.7 3.4 select_bitcast_fusion.3
  17.0 2.8 select_bitcast_fusion.2
  19.9 1.6 collective-permute-start.6
  21.5 3.3 collective-permute-start.7
  24.8 0.9 collective-permute-start.8
  25.7 0.6 fusion.44
  27.7 261.5 %collective-permute-start = (s32[1]{0:T(128)}, s32[1]{0:T(128)}, u32[]{:S(2)}, u32[]{:S(2)}) collective-permute-start(s32[1]{0:T(128)} %bitcast.4), channel_id=1, source_target_pairs={{0,3},{1,4},{2,5},{3,6},{4,7},{5,8},{6,9},{7,10},{8,11},{9,12},{10... | collective-permute-start | bytes 20 | tf_op jit(solution)/shard_map/ppermute | solution.py:13
  290.6 1.1 collective-permute-start.2
  294.3 4.8 collective-permute-start.4
  299.2 1.5 collective-permute-done.4
  300.7 2.0 add_convert_fusion
  302.6 0.1 fusion.37
  302.7 0.1 broadcast_in_dim.2
  302.8 0.1 mul.48
  304.8 0.0 copy-start.1
  304.8 3.9 fusion.10
  308.7 0.0 collective-permute-done.6
  308.7 0.0 collective-permute-done.7
  308.7 0.0 collective-permute-done.8
  308.7 0.0 copy-done.1
  308.7 0.0 copy-start.2
  308.7 4.0 pad_maximum_fusion
  312.7 0.0 copy-start.3
  312.7 1.2 fusion.22
  314.0 0.3 copy-done.3
  314.3 1.2 fusion.23
  315.6 4.4 fusion
  320.0 0.0 reduce-scatter.2.cloned.1.call-update
  320.0 4.0 fusion.9
  323.9 1.9 collective-permute-start.1
  325.8 1.1 collective-permute-start.3
  326.9 3.1 collective-permute-start.5
  331.3 128.4 %collective-permute-done.1 = bf16[2,64,8192]{2,1,0:T(8,128)(2,1)} collective-permute-done((bf16[2,64,8192]{2,1,0:T(8,128)(2,1)}, bf16[2,64,8192]{2,1,0:T(8,128)(2,1)}, u32[]{:S(2)}, u32[]{:S(2)}) %collective-permute-start.1) | collective-permute-done | bytes 2097184 | tf_op jit(solution)/shard_map/ppermute | solution.py:13
  459.7 66.2 %collective-permute-done.3 = bf16[2,64,8192]{2,1,0:T(8,128)(2,1)} collective-permute-done((bf16[2,64,8192]{2,1,0:T(8,128)(2,1)}, bf16[2,64,8192]{2,1,0:T(8,128)(2,1)}, u32[]{:S(2)}, u32[]{:S(2)}) %collective-permute-start.3) | collective-permute-done | bytes 2097184 | tf_op jit(solution)/shard_map/ppermute | solution.py:13
  525.9 73.5 %collective-permute-done.5 = bf16[2,64,8192]{2,1,0:T(8,128)(2,1)} collective-permute-done((bf16[2,64,8192]{2,1,0:T(8,128)(2,1)}, bf16[2,64,8192]{2,1,0:T(8,128)(2,1)}, u32[]{:S(2)}, u32[]{:S(2)}) %collective-permute-start.5) | collective-permute-done | bytes 2097184 | tf_op jit(solution)/shard_map/ppermute | solution.py:13
  599.3 5.0 fusion.14
  604.4 3.2 convolution_convert_fusion.1
  607.6 0.0 copy-start
  607.6 4.4 fusion.1
  612.0 3.6 convolution_convert_fusion
  615.6 3.6 fusion.2
  619.2 4.3 pad_maximum_fusion.3
  623.5 1.1 fusion.43
  624.6 0.8 copy.35
  625.4 0.8 copy.36
  (8 shorter events, 0.0 us)
Async XLA Ops:
  7.2 616.3 %reduce-scatter.2.cloned.1.call-start = ((), (), s32[]{:S(2)}) async-start(), calls=%async_computation.1 | async-start | bytes 4718592 | tf_op jit(solution)/shard_map/reduce_scatter | solution.py:124
  19.9 288.8 %collective-permute-start.6 = (bf16[2,64,8192]{2,1,0:T(8,128)(2,1)}, bf16[2,64,8192]{2,1,0:T(8,128)(2,1)}, u32[]{:S(2)}, u32[]{:S(2)}) collective-permute-start(bf16[2,64,8192]{2,1,0:T(8,128)(2,1)} %get-tuple-element.14), channel_id=1, source_target_pairs={{0,1},{1,2},{2,3},{3,4},{4,5},{5,6},{6,7},{7,8},{8,9},{9,10},{10,1... | collective-permute-start | bytes 6291464 | tf_op jit(solution)/shard_map/ppermute | solution.py:13
  21.5 287.2 %collective-permute-start.7 = (bf16[2,64,8192]{2,1,0:T(8,128)(2,1)}, bf16[2,64,8192]{2,1,0:T(8,128)(2,1)}, u32[]{:S(2)}, u32[]{:S(2)}) collective-permute-start(bf16[2,64,8192]{2,1,0:T(8,128)(2,1)} %get-tuple-element.15), channel_id=1, source_target_pairs={{0,2},{1,3},{2,4},{3,5},{4,6},{5,7},{6,8},{7,9},{8,10},{9,11},{10,... | collective-permute-start | bytes 6291464 | tf_op jit(solution)/shard_map/ppermute | solution.py:13
  24.8 283.9 %collective-permute-start.8 = (bf16[2,64,8192]{2,1,0:T(8,128)(2,1)}, bf16[2,64,8192]{2,1,0:T(8,128)(2,1)}, u32[]{:S(2)}, u32[]{:S(2)}) collective-permute-start(bf16[2,64,8192]{2,1,0:T(8,128)(2,1)} %get-tuple-element.16), channel_id=1, source_target_pairs={{0,3},{1,4},{2,5},{3,6},{4,7},{5,8},{6,9},{7,10},{8,11},{9,12},{10... | collective-permute-start | bytes 6291464 | tf_op jit(solution)/shard_map/ppermute | solution.py:13
  27.7 266.6 %collective-permute-start = (s32[1]{0:T(128)}, s32[1]{0:T(128)}, u32[]{:S(2)}, u32[]{:S(2)}) collective-permute-start(s32[1]{0:T(128)} %bitcast.4), channel_id=1, source_target_pairs={{0,3},{1,4},{2,5},{3,6},{4,7},{5,8},{6,9},{7,10},{8,11},{9,12},{10... | collective-permute-start | bytes 20 | tf_op jit(solution)/shard_map/ppermute | solution.py:13
  290.6 8.6 %collective-permute-start.2 = (s32[1]{0:T(128)}, s32[1]{0:T(128)}, u32[]{:S(2)}, u32[]{:S(2)}) collective-permute-start(s32[1]{0:T(128)} %bitcast.13), channel_id=1, source_target_pairs={{0,2},{1,3},{2,4},{3,5},{4,6},{5,7},{6,8},{7,9},{8,10},{9,11},{10,... | collective-permute-start | bytes 20 | tf_op jit(solution)/shard_map/ppermute | solution.py:13
  294.3 6.4 %collective-permute-start.4 = (s32[1]{0:T(128)}, s32[1]{0:T(128)}, u32[]{:S(2)}, u32[]{:S(2)}) collective-permute-start(s32[1]{0:T(128)} %bitcast.19), channel_id=1, source_target_pairs={{0,1},{1,2},{2,3},{3,4},{4,5},{5,6},{6,7},{7,8},{8,9},{9,10},{10,1... | collective-permute-start | bytes 20 | tf_op jit(solution)/shard_map/ppermute | solution.py:13
  304.8 3.9 copy-start.1
  308.7 4.0 copy-start.2
  312.7 1.6 copy-start.3
  323.9 135.8 %collective-permute-start.1 = (bf16[2,64,8192]{2,1,0:T(8,128)(2,1)}, bf16[2,64,8192]{2,1,0:T(8,128)(2,1)}, u32[]{:S(2)}, u32[]{:S(2)}) collective-permute-start(bf16[2,64,8192]{2,1,0:T(8,128)(2,1)} %get-tuple-element.18), channel_id=1, source_target_pairs={{0,29},{1,30},{2,31},{3,0},{4,1},{5,2},{6,3},{7,4},{8,5},{9,6},{10... | collective-permute-start | bytes 6291464 | tf_op jit(solution)/shard_map/ppermute | solution.py:13
  325.8 200.0 %collective-permute-start.3 = (bf16[2,64,8192]{2,1,0:T(8,128)(2,1)}, bf16[2,64,8192]{2,1,0:T(8,128)(2,1)}, u32[]{:S(2)}, u32[]{:S(2)}) collective-permute-start(bf16[2,64,8192]{2,1,0:T(8,128)(2,1)} %get-tuple-element.17), channel_id=1, source_target_pairs={{0,30},{1,31},{2,0},{3,1},{4,2},{5,3},{6,4},{7,5},{8,6},{9,7},{10,... | collective-permute-start | bytes 6291464 | tf_op jit(solution)/shard_map/ppermute | solution.py:13
  326.9 272.4 %collective-permute-start.5 = (bf16[2,64,8192]{2,1,0:T(8,128)(2,1)}, bf16[2,64,8192]{2,1,0:T(8,128)(2,1)}, u32[]{:S(2)}, u32[]{:S(2)}) collective-permute-start(bf16[2,64,8192]{2,1,0:T(8,128)(2,1)} %get-tuple-element.7), channel_id=1, source_target_pairs={{0,31},{1,0},{2,1},{3,2},{4,3},{5,4},{6,5},{7,6},{8,7},{9,8},{10,9... | collective-permute-start | bytes 6291464 | tf_op jit(solution)/shard_map/ppermute | solution.py:13
  607.6 4.4 copy-start
Sparse Core Ops, SparseCore 0:
  320.1 44.0 reduce-scatter.1

commit v4 on v3

--- a/solution.py
+++ b/solution.py
@@ -118,15 +118,13 @@
         ],
         axis=1,
     )
-    joined = jnp.einsum(
-        "nwjd,nwjc->dc", arrived, blocks_right, preferred_element_type=jnp.float32
-    ).astype(jnp.bfloat16)
+    joined = jnp.einsum("nwjd,nwjc->dc", arrived, blocks_right, preferred_element_type=jnp.float32)
     summed = lax.psum_scatter(joined, "dp", scatter_dimension=0, tiled=True)
     width = held_count * rank_size
     part_rows = summed.shape[0]
     grad_down = jnp.transpose(summed[:, :width].reshape(part_rows, held_count, rank_size), (1, 0, 2))
     grad_up = jnp.transpose(summed[:, width:].reshape(part_rows, held_count, rank_size), (1, 2, 0))
-    return (adapter_out, grad_tokens, grad_down, grad_up)
+    return (adapter_out, grad_tokens, grad_down.astype(jnp.bfloat16), grad_up.astype(jnp.bfloat16))
 
 
 def solution(mesh):

time: 635 us -> 634 us (level)
  no operation moved by 1% of the time
where the time goes in v4:
time: 634 us; the launch traced here: 632 us
  starting transfers between devices  279 us (44%)
  waiting for transfers between devices  270 us (43%)
  other arithmetic  28.6 us (5%)
  between operations  27.8 us (4%)
  matrix products  23.1 us (4%)
    ppermute x9, starting transfers between devices, shifted(): return lax.ppermute(value, axis, pairs)  279 us
    ppermute x9, waiting for transfers between devices, shifted(): return lax.ppermute(value, axis, pairs)  270 us
  transfers between devices with their start and end apart: 10, of which 4 were waited for; matrix products, arithmetic and copies ran while one was open for 5% of the time, Pallas kernels for 0%

profile of v4, /device:TPU:71, one launch (start us, length us, event | category | flops | bytes accessed | tf_op | source)
XLA Modules:
  0.0 632.0 jit_solution(13967886911086718760)
XLA Ops:
  7.2 0.0 reduce-scatter.2.cloned.1.call-start
  7.2 0.7 multiply_subtract_fusion
  7.9 0.6 fusion.44
  13.7 2.4 select_bitcast_fusion.3
  16.1 2.8 select_bitcast_fusion.2
  18.9 1.6 collective-permute-start.6
  20.5 3.3 collective-permute-start.7
  23.8 0.9 collective-permute-start.8
  24.7 0.7 fusion.43
  26.7 261.5 %collective-permute-start = (s32[1]{0:T(128)}, s32[1]{0:T(128)}, u32[]{:S(2)}, u32[]{:S(2)}) collective-permute-start(s32[1]{0:T(128)} %bitcast.4), channel_id=1, source_target_pairs={{0,3},{1,4},{2,5},{3,6},{4,7},{5,8},{6,9},{7,10},{8,11},{9,12},{10... | collective-permute-start | bytes 20 | tf_op jit(solution)/shard_map/ppermute | solution.py:13
  289.6 1.1 collective-permute-start.2
  293.3 4.8 collective-permute-start.4
  298.2 1.5 collective-permute-done.4
  299.7 1.9 add_convert_fusion
  301.6 0.1 fusion.36
  301.7 0.1 broadcast_in_dim.2
  301.8 0.1 mul.48
  301.9 0.0 collective-permute-done.6
  301.9 0.0 collective-permute-done.7
  301.9 0.0 collective-permute-done.8
  301.9 0.0 copy-start.3
  301.9 4.0 pad_maximum_fusion
  305.9 0.0 copy-done.3
  305.9 0.0 copy-start.2
  305.9 1.2 fusion.21
  307.2 0.3 copy-done.2
  307.5 1.4 fusion.22
  308.9 5.6 convolution_bitcast_fusion
  314.6 0.0 reduce-scatter.2.cloned.1.call-update
  316.5 3.3 fusion.9
  319.8 2.7 fusion.8
  322.5 0.0 copy-done
  322.5 1.9 collective-permute-start.1
  324.4 1.1 collective-permute-start.3
  325.5 3.1 collective-permute-start.5
  329.9 128.4 %collective-permute-done.1 = bf16[2,64,8192]{2,1,0:T(8,128)(2,1)} collective-permute-done((bf16[2,64,8192]{2,1,0:T(8,128)(2,1)}, bf16[2,64,8192]{2,1,0:T(8,128)(2,1)}, u32[]{:S(2)}, u32[]{:S(2)}) %collective-permute-start.1) | collective-permute-done | bytes 2097184 | tf_op jit(solution)/shard_map/ppermute | solution.py:13
  458.3 66.2 %collective-permute-done.3 = bf16[2,64,8192]{2,1,0:T(8,128)(2,1)} collective-permute-done((bf16[2,64,8192]{2,1,0:T(8,128)(2,1)}, bf16[2,64,8192]{2,1,0:T(8,128)(2,1)}, u32[]{:S(2)}, u32[]{:S(2)}) %collective-permute-start.3) | collective-permute-done | bytes 2097184 | tf_op jit(solution)/shard_map/ppermute | solution.py:13
  524.5 73.5 %collective-permute-done.5 = bf16[2,64,8192]{2,1,0:T(8,128)(2,1)} collective-permute-done((bf16[2,64,8192]{2,1,0:T(8,128)(2,1)}, bf16[2,64,8192]{2,1,0:T(8,128)(2,1)}, u32[]{:S(2)}, u32[]{:S(2)}) %collective-permute-start.5) | collective-permute-done | bytes 2097184 | tf_op jit(solution)/shard_map/ppermute | solution.py:13
  597.9 5.0 fusion.13
  603.0 3.2 convolution_convert_fusion.1
  606.2 0.0 copy-start.1
  606.2 4.4 fusion
  610.6 3.6 convolution_convert_fusion
  614.2 3.7 fusion.1
  617.8 4.3 pad_maximum_fusion.3
  622.1 1.3 convert.4
  623.5 0.9 copy.35
  624.3 0.8 copy.36
  (9 shorter events, 0.1 us)
Async XLA Ops:
  7.2 615.0 %reduce-scatter.2.cloned.1.call-start = ((), (), s32[]{:S(2)}) async-start(), calls=%async_computation.1 | async-start | bytes 9437184 | tf_op jit(solution)/shard_map/reduce_scatter | solution.py:122
  18.9 283.0 %collective-permute-start.6 = (bf16[2,64,8192]{2,1,0:T(8,128)(2,1)}, bf16[2,64,8192]{2,1,0:T(8,128)(2,1)}, u32[]{:S(2)}, u32[]{:S(2)}) collective-permute-start(bf16[2,64,8192]{2,1,0:T(8,128)(2,1)} %get-tuple-element.14), channel_id=1, source_target_pairs={{0,1},{1,2},{2,3},{3,4},{4,5},{5,6},{6,7},{7,8},{8,9},{9,10},{10,1... | collective-permute-start | bytes 6291464 | tf_op jit(solution)/shard_map/ppermute | solution.py:13
  20.5 281.4 %collective-permute-start.7 = (bf16[2,64,8192]{2,1,0:T(8,128)(2,1)}, bf16[2,64,8192]{2,1,0:T(8,128)(2,1)}, u32[]{:S(2)}, u32[]{:S(2)}) collective-permute-start(bf16[2,64,8192]{2,1,0:T(8,128)(2,1)} %get-tuple-element.15), channel_id=1, source_target_pairs={{0,2},{1,3},{2,4},{3,5},{4,6},{5,7},{6,8},{7,9},{8,10},{9,11},{10,... | collective-permute-start | bytes 6291464 | tf_op jit(solution)/shard_map/ppermute | solution.py:13
  23.8 278.1 %collective-permute-start.8 = (bf16[2,64,8192]{2,1,0:T(8,128)(2,1)}, bf16[2,64,8192]{2,1,0:T(8,128)(2,1)}, u32[]{:S(2)}, u32[]{:S(2)}) collective-permute-start(bf16[2,64,8192]{2,1,0:T(8,128)(2,1)} %get-tuple-element.16), channel_id=1, source_target_pairs={{0,3},{1,4},{2,5},{3,6},{4,7},{5,8},{6,9},{7,10},{8,11},{9,12},{10... | collective-permute-start | bytes 6291464 | tf_op jit(solution)/shard_map/ppermute | solution.py:13
  26.7 266.6 %collective-permute-start = (s32[1]{0:T(128)}, s32[1]{0:T(128)}, u32[]{:S(2)}, u32[]{:S(2)}) collective-permute-start(s32[1]{0:T(128)} %bitcast.4), channel_id=1, source_target_pairs={{0,3},{1,4},{2,5},{3,6},{4,7},{5,8},{6,9},{7,10},{8,11},{9,12},{10... | collective-permute-start | bytes 20 | tf_op jit(solution)/shard_map/ppermute | solution.py:13
  289.6 8.6 %collective-permute-start.2 = (s32[1]{0:T(128)}, s32[1]{0:T(128)}, u32[]{:S(2)}, u32[]{:S(2)}) collective-permute-start(s32[1]{0:T(128)} %bitcast.13), channel_id=1, source_target_pairs={{0,2},{1,3},{2,4},{3,5},{4,6},{5,7},{6,8},{7,9},{8,10},{9,11},{10,... | collective-permute-start | bytes 20 | tf_op jit(solution)/shard_map/ppermute | solution.py:13
  293.3 6.4 %collective-permute-start.4 = (s32[1]{0:T(128)}, s32[1]{0:T(128)}, u32[]{:S(2)}, u32[]{:S(2)}) collective-permute-start(s32[1]{0:T(128)} %bitcast.19), channel_id=1, source_target_pairs={{0,1},{1,2},{2,3},{3,4},{4,5},{5,6},{6,7},{7,8},{8,9},{9,10},{10,1... | collective-permute-start | bytes 20 | tf_op jit(solution)/shard_map/ppermute | solution.py:13
  301.9 4.0 copy-start.3
  305.9 1.6 copy-start.2
  319.8 2.7 copy-start
  322.5 135.8 %collective-permute-start.1 = (bf16[2,64,8192]{2,1,0:T(8,128)(2,1)}, bf16[2,64,8192]{2,1,0:T(8,128)(2,1)}, u32[]{:S(2)}, u32[]{:S(2)}) collective-permute-start(bf16[2,64,8192]{2,1,0:T(8,128)(2,1)} %get-tuple-element.18), channel_id=1, source_target_pairs={{0,29},{1,30},{2,31},{3,0},{4,1},{5,2},{6,3},{7,4},{8,5},{9,6},{10... | collective-permute-start | bytes 6291464 | tf_op jit(solution)/shard_map/ppermute | solution.py:13
  324.4 200.0 %collective-permute-start.3 = (bf16[2,64,8192]{2,1,0:T(8,128)(2,1)}, bf16[2,64,8192]{2,1,0:T(8,128)(2,1)}, u32[]{:S(2)}, u32[]{:S(2)}) collective-permute-start(bf16[2,64,8192]{2,1,0:T(8,128)(2,1)} %get-tuple-element.17), channel_id=1, source_target_pairs={{0,30},{1,31},{2,0},{3,1},{4,2},{5,3},{6,4},{7,5},{8,6},{9,7},{10,... | collective-permute-start | bytes 6291464 | tf_op jit(solution)/shard_map/ppermute | solution.py:13
  325.5 272.4 %collective-permute-start.5 = (bf16[2,64,8192]{2,1,0:T(8,128)(2,1)}, bf16[2,64,8192]{2,1,0:T(8,128)(2,1)}, u32[]{:S(2)}, u32[]{:S(2)}) collective-permute-start(bf16[2,64,8192]{2,1,0:T(8,128)(2,1)} %get-tuple-element.7), channel_id=1, source_target_pairs={{0,31},{1,0},{2,1},{3,2},{4,3},{5,4},{6,5},{7,6},{8,7},{9,8},{10,9... | collective-permute-start | bytes 6291464 | tf_op jit(solution)/shard_map/ppermute | solution.py:13
  606.2 4.4 copy-start.1
Sparse Core Ops, SparseCore 0:
  314.7 57.7 reduce-scatter.1

commit v5 on v4

--- a/solution.py
+++ b/solution.py
@@ -27,6 +27,8 @@
     seg_rows = tokens.shape[0] // segs_here
     reach_count = 2 * segs_here
     position = lax.axis_index("adapter")
+    every_seg = lax.all_gather(seg_adapter, "adapter", tiled=True)
+    seg_adapter = lax.dynamic_slice(every_seg, (position * segs_here,), (segs_here,))
     owners_of = seg_adapter // held_count
     local_index = seg_adapter - owners_of * held_count
     distance = jnp.mod(owners_of - position, groups)
@@ -49,7 +51,13 @@
     sel_list = [selector_of(k) for k in range(reach_count)]
     arrived_sel = [sel_list[0]]
     for k in range(1, reach_count):
-        arrived_sel.append(shifted(sel_list[k], "adapter", k))
+        asker = jnp.mod(position - k, groups)
+        asked = lax.dynamic_slice(every_seg, (asker * segs_here,), (segs_here,))
+        asked_owner = asked // held_count
+        sel = jnp.int32(-1)
+        for seg in range(segs_here):
+            sel = jnp.where(asked_owner[seg] == position, asked[seg] - asked_owner[seg] * held_count, sel)
+        arrived_sel.append(sel.reshape(1))
 
     both_blocks = jnp.stack([token_blocks, grad_blocks], axis=1)
     pay_list = [slot_of(both_blocks, k) for k in range(reach_count)]

time: 634 us -> 633 us (level)
  starting transfers between devices: 279 us -> 8.98 us
  waiting for transfers between devices: 270 us -> 512 us
  blocking collectives: 0 us -> 17.6 us
  between operations: 27.8 us -> 34.2 us
    ppermute x9 -> x6, starting transfers between devices: 279 us -> 8.94 us  [shifted(): return lax.ppermute(value, axis, pairs)]
    ppermute x9 -> x6, waiting for transfers between devices: 270 us -> 512 us  [shifted(): return lax.ppermute(value, axis, pairs)]
    unnamed x0 -> x1, blocking collectives: none -> 17.6 us
  transfers between devices with their start and end apart: 10 -> 7, of which waited for: 4 -> 6; matrix products, arithmetic and copies ran while one was open for 5% -> 5% of each run, Pallas kernels for 0% -> 0%
where the time goes in v5:
time: 633 us; the launch traced here: 630 us
  waiting for transfers between devices  512 us (81%)
  between operations  34.2 us (5%)
  other arithmetic  26.5 us (4%)
  matrix products  23.1 us (4%)
  blocking collectives  17.6 us (3%)
  starting transfers between devices  8.98 us (1%)
  local copies, waits for them, and re-layouts  7.49 us (1%)
    ppermute x6, waiting for transfers between devices, shifted(): return lax.ppermute(value, axis, pairs)  512 us
    unnamed x1, blocking collectives  17.6 us
  transfers between devices with their start and end apart: 7, of which 6 were waited for; matrix products, arithmetic and copies ran while one was open for 5% of the time, Pallas kernels for 0%

profile of v5, /device:TPU:71, one launch (start us, length us, event | category | flops | bytes accessed | tf_op | source)
XLA Modules:
  0.0 630.0 jit_solution(11898157272324763308)
XLA Ops:
  7.2 0.0 reduce-scatter.2.cloned.1.call-start
  7.3 1.3 dynamic-slice
  9.2 0.9 dynamic-update-slice
  10.0 17.6 %all-reduce.2 = s32[64]{0:T(128)S(1)} all-reduce(s32[64]{0:T(128)S(1)} %dynamic-update-slice), channel_id=1, replica_groups=mesh['dp'=8,'adapter'=32] {'adapter'}, use_global_device_ids=true, to_apply=%add.2 | all-reduce | flops 64 | bytes 512
  27.7 0.1 and_select_fusion.3
  27.8 0.7 fusion.43
  33.6 2.4 select_bitcast_fusion.3
  36.0 2.8 select_bitcast_fusion.2
  38.9 0.8 collective-permute-start.3
  39.6 0.2 collective-permute-start.4
  39.9 3.3 collective-permute-start.5
  43.2 0.1 and_select_fusion.1
  43.3 0.6 fusion.46
  46.5 0.7 fusion.48
  49.7 0.6 fusion.50
  52.9 0.6 fusion.44
  58.6 0.1 add_convert_fusion
  58.7 0.1 fusion.36
  58.8 0.1 broadcast_in_dim.2
  58.9 0.1 mul.88
  59.0 22.4 %collective-permute-done.3 = bf16[2,64,8192]{2,1,0:T(8,128)(2,1)} collective-permute-done((bf16[2,64,8192]{2,1,0:T(8,128)(2,1)}, bf16[2,64,8192]{2,1,0:T(8,128)(2,1)}, u32[]{:S(2)}, u32[]{:S(2)}) %collective-permute-start.3) | collective-permute-done | bytes 2097184 | tf_op jit(solution)/shard_map/ppermute | solution.py:13
  81.3 56.9 %collective-permute-done.4 = bf16[2,64,8192]{2,1,0:T(8,128)(2,1)} collective-permute-done((bf16[2,64,8192]{2,1,0:T(8,128)(2,1)}, bf16[2,64,8192]{2,1,0:T(8,128)(2,1)}, u32[]{:S(2)}, u32[]{:S(2)}) %collective-permute-start.4) | collective-permute-done | bytes 2097184 | tf_op jit(solution)/shard_map/ppermute | solution.py:13
  138.3 166.3 %collective-permute-done.5 = bf16[2,64,8192]{2,1,0:T(8,128)(2,1)} collective-permute-done((bf16[2,64,8192]{2,1,0:T(8,128)(2,1)}, bf16[2,64,8192]{2,1,0:T(8,128)(2,1)}, u32[]{:S(2)}, u32[]{:S(2)}) %collective-permute-start.5) | collective-permute-done | bytes 2097184 | tf_op jit(solution)/shard_map/ppermute | solution.py:13
  304.6 4.0 pad_maximum_fusion
  308.6 0.0 copy-start.4
  308.6 1.2 fusion.22
  309.9 0.3 copy-done.4
  310.2 1.4 fusion.21
  311.6 5.6 convolution_bitcast_fusion
  317.2 0.0 reduce-scatter.2.cloned.1.call-update
  317.2 3.3 fusion.9
  320.6 2.7 fusion.8
  323.3 0.0 collective-permute-start
  323.3 4.6 collective-permute-start.1
  327.9 0.0 collective-permute-start.2
  329.2 124.4 %collective-permute-done = bf16[2,64,8192]{2,1,0:T(8,128)(2,1)} collective-permute-done((bf16[2,64,8192]{2,1,0:T(8,128)(2,1)}, bf16[2,64,8192]{2,1,0:T(8,128)(2,1)}, u32[]{:S(2)}, u32[]{:S(2)}) %collective-permute-start) | collective-permute-done | bytes 2097184 | tf_op jit(solution)/shard_map/ppermute | solution.py:13
  453.5 86.3 %collective-permute-done.1 = bf16[2,64,8192]{2,1,0:T(8,128)(2,1)} collective-permute-done((bf16[2,64,8192]{2,1,0:T(8,128)(2,1)}, bf16[2,64,8192]{2,1,0:T(8,128)(2,1)}, u32[]{:S(2)}, u32[]{:S(2)}) %collective-permute-start.1) | collective-permute-done | bytes 2097184 | tf_op jit(solution)/shard_map/ppermute | solution.py:13
  539.8 55.7 %collective-permute-done.2 = bf16[2,64,8192]{2,1,0:T(8,128)(2,1)} collective-permute-done((bf16[2,64,8192]{2,1,0:T(8,128)(2,1)}, bf16[2,64,8192]{2,1,0:T(8,128)(2,1)}, u32[]{:S(2)}, u32[]{:S(2)}) %collective-permute-start.2) | collective-permute-done | bytes 2097184 | tf_op jit(solution)/shard_map/ppermute | solution.py:13
  595.6 5.0 fusion.13
  600.6 4.2 convolution_convert_fusion.1
  604.8 3.4 fusion
  608.2 3.7 convolution_convert_fusion
  611.9 3.6 fusion.1
  615.5 3.1 pad_maximum_fusion.4
  618.6 1.5 pad_maximum_fusion.3
  620.1 1.3 convert.4
  621.5 0.9 copy.35
  622.3 0.8 copy.36
  (14 shorter events, 0.1 us)
Async XLA Ops:
  7.2 613.0 %reduce-scatter.2.cloned.1.call-start = ((), (), s32[]{:S(2)}) async-start(), calls=%async_computation.1 | async-start | bytes 9437184 | tf_op jit(solution)/shard_map/reduce_scatter | solution.py:130
  38.9 42.5 %collective-permute-start.3 = (bf16[2,64,8192]{2,1,0:T(8,128)(2,1)}, bf16[2,64,8192]{2,1,0:T(8,128)(2,1)}, u32[]{:S(2)}, u32[]{:S(2)}) collective-permute-start(bf16[2,64,8192]{2,1,0:T(8,128)(2,1)} %get-tuple-element.20), channel_id=1, source_target_pairs={{0,1},{1,2},{2,3},{3,4},{4,5},{5,6},{6,7},{7,8},{8,9},{9,10},{10,1... | collective-permute-start | bytes 6291464 | tf_op jit(solution)/shard_map/ppermute | solution.py:13
  39.6 98.6 %collective-permute-start.4 = (bf16[2,64,8192]{2,1,0:T(8,128)(2,1)}, bf16[2,64,8192]{2,1,0:T(8,128)(2,1)}, u32[]{:S(2)}, u32[]{:S(2)}) collective-permute-start(bf16[2,64,8192]{2,1,0:T(8,128)(2,1)} %get-tuple-element.21), channel_id=1, source_target_pairs={{0,2},{1,3},{2,4},{3,5},{4,6},{5,7},{6,8},{7,9},{8,10},{9,11},{10,... | collective-permute-start | bytes 6291464 | tf_op jit(solution)/shard_map/ppermute | solution.py:13
  39.9 264.7 %collective-permute-start.5 = (bf16[2,64,8192]{2,1,0:T(8,128)(2,1)}, bf16[2,64,8192]{2,1,0:T(8,128)(2,1)}, u32[]{:S(2)}, u32[]{:S(2)}) collective-permute-start(bf16[2,64,8192]{2,1,0:T(8,128)(2,1)} %get-tuple-element.22), channel_id=1, source_target_pairs={{0,3},{1,4},{2,5},{3,6},{4,7},{5,8},{6,9},{7,10},{8,11},{9,12},{10... | collective-permute-start | bytes 6291464 | tf_op jit(solution)/shard_map/ppermute | solution.py:13
  304.6 4.0 copy-start.3
  308.6 1.6 copy-start.4
  320.6 2.7 copy-start
  323.3 130.2 %collective-permute-start = (bf16[2,64,8192]{2,1,0:T(8,128)(2,1)}, bf16[2,64,8192]{2,1,0:T(8,128)(2,1)}, u32[]{:S(2)}, u32[]{:S(2)}) collective-permute-start(bf16[2,64,8192]{2,1,0:T(8,128)(2,1)} %get-tuple-element.24), channel_id=1, source_target_pairs={{0,29},{1,30},{2,31},{3,0},{4,1},{5,2},{6,3},{7,4},{8,5},{9,6},{10... | collective-permute-start | bytes 6291464 | tf_op jit(solution)/shard_map/ppermute | solution.py:13
  323.3 216.5 %collective-permute-start.1 = (bf16[2,64,8192]{2,1,0:T(8,128)(2,1)}, bf16[2,64,8192]{2,1,0:T(8,128)(2,1)}, u32[]{:S(2)}, u32[]{:S(2)}) collective-permute-start(bf16[2,64,8192]{2,1,0:T(8,128)(2,1)} %get-tuple-element.23), channel_id=1, source_target_pairs={{0,30},{1,31},{2,0},{3,1},{4,2},{5,3},{6,4},{7,5},{8,6},{9,7},{10,... | collective-permute-start | bytes 6291464 | tf_op jit(solution)/shard_map/ppermute | solution.py:13
  327.9 267.7 %collective-permute-start.2 = (bf16[2,64,8192]{2,1,0:T(8,128)(2,1)}, bf16[2,64,8192]{2,1,0:T(8,128)(2,1)}, u32[]{:S(2)}, u32[]{:S(2)}) collective-permute-start(bf16[2,64,8192]{2,1,0:T(8,128)(2,1)} %get-tuple-element.9), channel_id=1, source_target_pairs={{0,31},{1,0},{2,1},{3,2},{4,3},{5,4},{6,5},{7,6},{8,7},{9,8},{10,9... | collective-permute-start | bytes 6291464 | tf_op jit(solution)/shard_map/ppermute | solution.py:13
  604.8 3.4 copy-start.1
  615.5 3.1 copy-start.2
Sparse Core Ops, SparseCore 0:
  317.3 60.3 reduce-scatter.1

commit v6 on v2

--- a/solution.py
+++ b/solution.py
@@ -52,7 +52,8 @@
         arrived_sel.append(shifted(sel_list[k], "adapter", k))
 
     both_blocks = jnp.stack([token_blocks, grad_blocks], axis=1)
-    pay_list = [slot_of(both_blocks, k) for k in range(reach_count)]
+    sent_list = [slot_of(both_blocks, k) for k in range(reach_count)]
+    pay_list = list(sent_list)
     for k in range(1, reach_count):
         pay_list[k] = shifted(pay_list[k], "adapter", k)
 
@@ -62,61 +63,77 @@
     for k in range(1, reach_count):
         wt_back[k] = shifted(pick(arrived_sel[k][0], panel_list, panel_list[0]), "adapter", -k)
 
-    outs = []
-    backs = []
     contract_last = (((1,), (1,)), ((), ()))
-    for seg in range(segs_here):
-        seg_panels = pick(local_index[seg], panel_list, panel_list[0])
-        for k in range(1, reach_count):
-            seg_panels = jnp.where(distance[seg] == k, wt_back[k], seg_panels)
-        seg_down_t = seg_panels[0]
-        seg_up = seg_panels[1]
+    slot_out = []
+    slot_back = []
+    for k in range(reach_count):
+        if k == 0:
+            panels = pick(sel_list[0][0], panel_list, panel_list[0])
+        else:
+            panels = wt_back[k]
+        rows_k = sent_list[k][0]
+        grads_k = sent_list[k][1]
         hidden = lax.dot_general(
-            token_blocks[seg], seg_down_t, contract_last, preferred_element_type=jnp.float32
+            rows_k, panels[0], contract_last, preferred_element_type=jnp.float32
         ).astype(jnp.bfloat16)
-        outs.append(
-            (adapter_scale * jnp.dot(hidden, seg_up, preferred_element_type=jnp.float32)).astype(
+        slot_out.append(
+            (adapter_scale * jnp.dot(hidden, panels[1], preferred_element_type=jnp.float32)).astype(
                 jnp.bfloat16
             )
         )
         hidden_grad = (
             adapter_scale
-            * lax.dot_general(
-                grad_blocks[seg], seg_up, contract_last, preferred_element_type=jnp.float32
-            )
+            * lax.dot_general(grads_k, panels[1], contract_last, preferred_element_type=jnp.float32)
         ).astype(jnp.bfloat16)
-        backs.append(
-            jnp.dot(hidden_grad, seg_down_t, preferred_element_type=jnp.float32).astype(jnp.bfloat16)
+        slot_back.append(
+            jnp.dot(hidden_grad, panels[0], preferred_element_type=jnp.float32).astype(jnp.bfloat16)
         )
-    adapter_out = jnp.concatenate(outs, axis=0)
-    grad_tokens = jnp.concatenate(backs, axis=0)
+    adapter_out = jnp.concatenate(
+        [pick(distance[seg], slot_out, slot_out[0]) for seg in range(segs_here)], axis=0
+    )
+    grad_tokens = jnp.concatenate(
+        [pick(distance[seg], slot_back, slot_back[0]) for seg in range(segs_here)], axis=0
+    )
 
-    arrived = jnp.stack(pay_list)
-    arrived_rows = arrived[:, 0]
-    arrived_grads = arrived[:, 1]
-    arrived_select = jnp.concatenate(arrived_sel).astype(jnp.float32)
-    picks = (
-        arrived_select[:, None] == jnp.arange(held_count, dtype=jnp.float32)[None, :]
-    ).astype(jnp.float32)
-    masking = jnp.repeat(picks, rank_size, axis=1)[:, None, :]
     down_cat = jnp.transpose(down_panels, (1, 0, 2)).reshape(feat_width, held_count * rank_size)
     up_weight_joined = up_panels.reshape(held_count * rank_size, feat_width)
-    hidden_state = (
-        jnp.einsum("njd,dc->njc", arrived_rows, down_cat, preferred_element_type=jnp.float32)
-        * masking
-    ).astype(jnp.bfloat16)
-    hidden_gradient = adapter_scale * jnp.einsum(
-        "njd,cd->njc", arrived_grads, up_weight_joined, preferred_element_type=jnp.float32
+
+    def right_blocks(arrived, select):
+        picks = (
+            select.astype(jnp.float32)[:, None] == jnp.arange(held_count, dtype=jnp.float32)[None, :]
+        ).astype(jnp.float32)
+        masking = jnp.repeat(picks, rank_size, axis=1)[:, None, :]
+        hidden_state = (
+            jnp.einsum("njd,dc->njc", arrived[:, 0], down_cat, preferred_element_type=jnp.float32)
+            * masking
+        ).astype(jnp.bfloat16)
+        hidden_gradient = adapter_scale * jnp.einsum(
+            "njd,cd->njc", arrived[:, 1], up_weight_joined, preferred_element_type=jnp.float32
+        )
+        hidden_gradient = (hidden_gradient * masking).astype(jnp.bfloat16)
+        zero_half = jnp.zeros_like(hidden_gradient)
+        doubled_hidden = (adapter_scale * hidden_state.astype(jnp.float32)).astype(jnp.bfloat16)
+        return jnp.stack(
+            [
+                jnp.concatenate([hidden_gradient, zero_half], axis=-1),
+                jnp.concatenate([zero_half, doubled_hidden], axis=-1),
+            ],
+            axis=1,
+        )
+
+    early = jnp.stack(pay_list[:-1])
+    early_sel = jnp.concatenate(arrived_sel[:-1])
+    joined = jnp.einsum(
+        "nwjd,nwjc->dc", early, right_blocks(early, early_sel), preferred_element_type=jnp.float32
     )
-    hidden_gradient = (hidden_gradient * masking).astype(jnp.bfloat16)
-    down_sum = jnp.einsum(
-        "njd,njc->dc", arrived_rows, hidden_gradient, preferred_element_type=jnp.float32
+    summed = lax.psum_scatter(joined, "dp", scatter_dimension=0, tiled=True)
+    late = pay_list[-1]
+    late_right = right_blocks(late[None], arrived_sel[-1])[0]
+    late_rows = lax.all_to_all(late, "dp", 2, 0, tiled=True)
+    late_right_all = lax.all_gather(late_right, "dp", axis=0, tiled=True)
+    summed = summed + jnp.einsum(
+        "mjd,mjc->dc", late_rows, late_right_all, preferred_element_type=jnp.float32
     )
-    up_sum_t = adapter_scale * jnp.einsum(
-        "njd,njc->dc", arrived_grads, hidden_state, preferred_element_type=jnp.float32
-    )
-    joined = jnp.concatenate([down_sum, up_sum_t], axis=1)
-    summed = lax.psum_scatter(joined, "dp", scatter_dimension=0, tiled=True)
     width = held_count * rank_size
     part_rows = summed.shape[0]
     grad_down = jnp.transpose(summed[:, :width].reshape(part_rows, held_count, rank_size), (1, 0, 2))

time: 653 us -> 515 us (0.79); the launches traced: 651 us -> 506 us
  starting transfers between devices: 280 us -> 159 us
  waiting for transfers between devices: 270 us -> 184 us
  local copies, waits for them, and re-layouts: 2.22 us -> 35.1 us
  blocking collectives: 0 us -> 28.8 us
  other arithmetic: 39.9 us -> 22.7 us
  matrix products: 32.3 us -> 49 us
    ppermute x9, starting transfers between devices: 280 us -> 150 us  [shifted(): return lax.ppermute(value, axis, pairs)]
    ppermute x9, waiting for transfers between devices: 270 us -> 184 us  [shifted(): return lax.ppermute(value, axis, pairs)]
    all_gather x0 -> x1, blocking collectives: none -> 28.8 us  [on_device(): late_right_all = lax.all_gather(late_right, 'dp', axis=0, tiled=True)]
    dot_general x6 -> x14, matrix products: 32.3 us -> 49 us  [the longest x4 17.9 us: on_device(): jnp.dot(hidden, panels[1], preferred_element_type=jnp.float32)]
    unnamed x6 -> x10, local copies, waits for them, and re-layouts: 0.02 us -> 13.2 us
    ppermute x0 -> x1, local copies, waits for them, and re-layouts: none -> 9.48 us  [shifted(): return lax.ppermute(value, axis, pairs)]
    all_to_all x0 -> x1, starting transfers between devices: none -> 9.15 us  [on_device(): late_rows = lax.all_to_all(late, 'dp', 2, 0, tiled=True)]
    all_to_all x0 -> x1, local copies, waits for them, and re-layouts: none -> 9.09 us  [on_device(): late_rows = lax.all_to_all(late, 'dp', 2, 0, tiled=True)]
  transfers between devices with their start and end apart: 10 -> 11, of which waited for: 4 -> 3; matrix products, arithmetic and copies ran while one was open for 5% -> 17% of each run, Pallas kernels for 0% -> 0%
where the time goes in v6:
time: 515 us; the launch traced here: 506 us
  waiting for transfers between devices  184 us (36%)
  starting transfers between devices  159 us (31%)
  matrix products  49 us (10%)
  local copies, waits for them, and re-layouts  35.1 us (7%)
  blocking collectives  28.8 us (6%)
  between operations  27.3 us (5%)
  other arithmetic  22.7 us (4%)
    ppermute x9, waiting for transfers between devices, shifted(): return lax.ppermute(value, axis, pairs)  184 us
    ppermute x9, starting transfers between devices, shifted(): return lax.ppermute(value, axis, pairs)  150 us
    all_gather x1, blocking collectives, on_device(): late_right_all = lax.all_gather(late_right, 'dp', axis=0, tiled=True)  28.8 us
    dot_general x4, matrix products, on_device(): jnp.dot(hidden, panels[1], preferred_element_type=jnp.float32)  17.9 us
    dot_general x4, matrix products, on_device(): jnp.dot(hidden_grad, panels[0], preferred_element_type=jnp.float32)  16.6 us
    unnamed x10, local copies, waits for them, and re-layouts  13.2 us
  transfers between devices with their start and end apart: 11, of which 3 were waited for; matrix products, arithmetic and copies ran while one was open for 17% of the time, Pallas kernels for 0%

profile of v6, /device:TPU:71, one launch (start us, length us, event | category | flops | bytes accessed | tf_op | source)
XLA Modules:
  0.0 505.7 jit_solution(9865500880109261187)
XLA Ops:
  7.2 0.7 multiply_subtract_fusion
  7.9 0.6 fusion.43
  13.7 2.4 select_select_fusion
  16.1 2.8 select_select_fusion.1
  18.9 4.2 collective-permute-start.7
  23.1 0.7 collective-permute-start.6
  23.8 0.6 fusion.42
  25.8 132.3 %collective-permute-start.4 = (s32[1]{0:T(128)}, s32[1]{0:T(128)}, u32[]{:S(2)}, u32[]{:S(2)}) collective-permute-start(s32[1]{0:T(128)} %bitcast.26), channel_id=1, source_target_pairs={{0,1},{1,2},{2,3},{3,4},{4,5},{5,6},{6,7},{7,8},{8,9},{9,10},{10,1... | collective-permute-start | bytes 20 | tf_op jit(solution)/shard_map/ppermute | solution.py:13
  159.5 1.5 collective-permute-start.2
  162.4 0.5 collective-permute-done.2
  162.8 1.3 add_convert_fusion.1
  164.1 0.1 fusion.33
  164.2 0.1 mul.89
  164.3 3.3 pad_maximum_fusion
  167.7 1.0 fusion.14
  168.7 0.6 copy-done.1
  169.3 1.0 fusion.15
  170.3 5.7 %convolution_bitcast_fusion = f32[8192,256]{1,0:T(8,128)} fusion(bf16[3,2,64,8192]{3,2,0,1:T(8,128)(2,1)S(1)} %pad_maximum_fusion, bf16[3,1,64,256]{3,2,0,1:T(8,128)(2,1)S(1)} %get-tuple-element.28, bf16[3,1,64,256]{3,2,0,1:T(8,128)(2,1)S(1)} %get-tuple-element.29), kind=kOutput, calls=%fused_computation | convolution fusion | flops 1610711040 | bytes 14876672 | tf_op jit(solution)/shard_map/nwjd,nwjc->dc/dot_general | solution.py:126
  177.4 3.7 collective-permute-start
  181.1 2.5 collective-permute-start.8
  183.6 3.3 broadcast_select_fusion
  188.9 3.1 select_bitcast_fusion
  192.0 3.9 fusion.3
  195.9 4.4 collective-permute-start.5
  200.3 2.9 convolution_convert_fusion
  203.2 0.2 collective-permute-start.1
  204.2 0.1 broadcast_in_dim.20
  204.3 113.2 %collective-permute-done.8 = bf16[2,64,8192]{2,1,0:T(8,128)(2,1)} collective-permute-done((bf16[2,64,8192]{2,1,0:T(8,128)(2,1)}, bf16[2,64,8192]{2,1,0:T(8,128)(2,1)}, u32[]{:S(2)}, u32[]{:S(2)}) %collective-permute-start.8) | collective-permute-done | bytes 2097184 | tf_op jit(solution)/shard_map/ppermute | solution.py:13
  317.5 9.5 %copy.32 = bf16[2,64,8192]{1,0,2:T(2,128)(2,1)} copy(bf16[2,64,8192]{2,1,0:T(8,128)(2,1)} %collective-permute-done.8) | data formatting | bytes 4194304 | tf_op jit(solution)/shard_map/ppermute | solution.py:13
  327.0 7.6 %reshape.164 = bf16[8,2,65536]{2,1,0:T(2,128)(2,1)} reshape(bf16[8192,2,64]{2,1,0:T(2,128)(2,1)} %bitcast.198) | data formatting | bytes 4194304
  334.6 9.1 %all-to-all-start = ((bf16[8,2,65536]{2,1,0:T(2,128)(2,1)}), bf16[8,2,65536]{2,1,0:T(2,128)(2,1)S(1)}, u32[]{:S(2)}, u32[]{:S(2)}) async-start(bf16[8,2,65536]{2,1,0:T(2,128)(2,1)} %reshape.164), calls=%async_computation.1 | async-start | bytes 4194304 | tf_op jit(solution)/shard_map/all_to_all | solution.py:132
  343.7 2.9 fusion.25
  346.6 2.1 fusion.26
  348.8 28.8 %all-gather = bf16[1,16,64,256]{3,2,0,1:T(8,128)(2,1)} all-gather(bf16[1,2,64,256]{3,2,0,1:T(8,128)(2,1)S(1)} %maximum_bitcast_fusion), channel_id=2, replica_groups=mesh['dp'=8,'adapter'=32] {'dp'}, dimensions={1}, use_global_device_ids=true | all-gather | bytes 589824 | tf_op jit(solution)/shard_map/all_gather | solution.py:133
  377.6 4.2 fusion.1
  381.8 4.2 convolution_convert_fusion.2
  385.9 4.1 convolution_convert_fusion.1
  390.1 70.1 %collective-permute-done.1 = bf16[2,64,8192]{2,1,0:T(8,128)(2,1)} collective-permute-done((bf16[2,64,8192]{2,1,0:T(8,128)(2,1)}, bf16[2,64,8192]{2,1,0:T(8,128)(2,1)}, u32[]{:S(2)}, u32[]{:S(2)}) %collective-permute-start.1) | collective-permute-done | bytes 2097184 | tf_op jit(solution)/shard_map/ppermute | solution.py:13
  460.2 5.4 %select_select_fusion.5 = (bf16[64,8192]{1,0:T(8,128)(2,1)}, bf16[64,8192]{1,0:T(8,128)(2,1)}) fusion(bf16[64,8192]{1,0:T(8,128)(2,1)} %convolution_convert_fusion.2, bf16[64,8192]{1,0:T(8,128)(2,1)} %convolution_convert_fusion.1, bf16[64,8192]{1,0:T(8,128)(2,1)S(1)} %convolution_convert_fusion, pred[]{:T(512)} %bitcast.23, pred[]{:T(512)} %bitcast.15, ...), kind=kOutput, calls=%fused_computation.86 | convolution fusion | flops 137895936 | bytes 8391680 | tf_op jit(solution)/shard_map/dot_general | solution.py:89
  465.6 4.1 fusion.2
  469.8 5.7 %select_select_fusion.7 = (bf16[64,8192]{1,0:T(8,128)(2,1)}, bf16[64,8192]{1,0:T(8,128)(2,1)}) fusion(bf16[64,8192]{1,0:T(8,128)(2,1)} %fusion.1, bf16[64,8192]{1,0:T(8,128)(2,1)} %fusion.2, bf16[64,8192]{1,0:T(8,128)(2,1)} %fusion.3, pred[]{:T(512)} %bitcast.23, pred[]{:T(512)} %bitcast.15, pred[]{:T(512)} %bitcast, pred[]{:T(512)} %bitcast.24, ...), kind=kOutput, calls=%fused_computation.88 | convolution fusion | flops 138416128 | bytes 8391680 | tf_op jit(solution)/shard_map/dot_general | solution.py:80
  475.5 4.3 pad_maximum_fusion.3
  479.8 5.1 reshape.165
  484.8 9.1 %copy.33 = bf16[2,64,8,1024]{3,1,0,2:T(8,128)(2,1)S(1)} copy(bf16[2,64,8,1024]{1,0,3,2:T(2,128)(2,1)} %bitcast.197) | data formatting | bytes 4194304 | tf_op jit(solution)/shard_map/all_to_all | solution.py:132
  493.9 1.8 convolution_bitcast_fusion.1
  495.8 1.3 add_convert_fusion
  497.1 0.8 copy.36
  498.0 0.8 copy.37
  (28 shorter events, 0.4 us)
Async XLA Ops:
  7.2 488.6 %reduce-scatter.2.cloned.1.call-start = ((), (), s32[]{:S(2)}) async-start(), calls=%async_computation.2 | async-start | bytes 9437184 | tf_op jit(solution)/shard_map/reduce_scatter | solution.py:129
  18.9 145.4 %collective-permute-start.7 = (bf16[2,64,8192]{2,1,0:T(8,128)(2,1)}, bf16[2,64,8192]{2,1,0:T(8,128)(2,1)}, u32[]{:S(2)}, u32[]{:S(2)}) collective-permute-start(bf16[2,64,8192]{2,1,0:T(8,128)(2,1)} %bitcast.44), channel_id=1, source_target_pairs={{0,2},{1,3},{2,4},{3,5},{4,6},{5,7},{6,8},{7,9},{8,10},{9,11},{10,... | collective-permute-start | bytes 6291464 | tf_op jit(solution)/shard_map/ppermute | solution.py:13
  23.1 141.2 %collective-permute-start.6 = (bf16[2,64,8192]{2,1,0:T(8,128)(2,1)}, bf16[2,64,8192]{2,1,0:T(8,128)(2,1)}, u32[]{:S(2)}, u32[]{:S(2)}) collective-permute-start(bf16[2,64,8192]{2,1,0:T(8,128)(2,1)} %bitcast.41), channel_id=1, source_target_pairs={{0,1},{1,2},{2,3},{3,4},{4,5},{5,6},{6,7},{7,8},{8,9},{9,10},{10,1... | collective-permute-start | bytes 6291464 | tf_op jit(solution)/shard_map/ppermute | solution.py:13
  25.8 136.5 %collective-permute-start.4 = (s32[1]{0:T(128)}, s32[1]{0:T(128)}, u32[]{:S(2)}, u32[]{:S(2)}) collective-permute-start(s32[1]{0:T(128)} %bitcast.26), channel_id=1, source_target_pairs={{0,1},{1,2},{2,3},{3,4},{4,5},{5,6},{6,7},{7,8},{8,9},{9,10},{10,1... | collective-permute-start | bytes 20 | tf_op jit(solution)/shard_map/ppermute | solution.py:13
  159.5 3.3 collective-permute-start.2
  164.3 3.4 copy-start
  167.7 1.6 copy-start.1
  177.4 10.8 %collective-permute-start = (s32[1]{0:T(128)}, s32[1]{0:T(128)}, u32[]{:S(2)}, u32[]{:S(2)}) collective-permute-start(s32[1]{0:T(128)} %bitcast.7), channel_id=1, source_target_pairs={{0,3},{1,4},{2,5},{3,6},{4,7},{5,8},{6,9},{7,10},{8,11},{9,12},{10... | collective-permute-start | bytes 20 | tf_op jit(solution)/shard_map/ppermute | solution.py:13
  181.1 136.4 %collective-permute-start.8 = (bf16[2,64,8192]{2,1,0:T(8,128)(2,1)}, bf16[2,64,8192]{2,1,0:T(8,128)(2,1)}, u32[]{:S(2)}, u32[]{:S(2)}) collective-permute-start(bf16[2,64,8192]{2,1,0:T(8,128)(2,1)} %bitcast.209), channel_id=1, source_target_pairs={{0,3},{1,4},{2,5},{3,6},{4,7},{5,8},{6,9},{7,10},{8,11},{9,12},{10... | collective-permute-start | bytes 6291464 | tf_op jit(solution)/shard_map/ppermute | solution.py:13
  192.0 185.6 %collective-permute-start.3 = (bf16[2,64,8192]{2,1,0:T(8,128)(2,1)}, bf16[2,64,8192]{2,1,0:T(8,128)(2,1)}, u32[]{:S(2)}, u32[]{:S(2)}) collective-permute-start(bf16[2,64,8192]{2,1,0:T(8,128)(2,1)} %get-tuple-element.17), channel_id=1, source_target_pairs={{0,30},{1,31},{2,0},{3,1},{4,2},{5,3},{6,4},{7,5},{8,6},{9,7},{10,... | collective-permute-start | bytes 6291464 | tf_op jit(solution)/shard_map/ppermute | solution.py:13
  195.9 190.1 %collective-permute-start.5 = (bf16[2,64,8192]{2,1,0:T(8,128)(2,1)}, bf16[2,64,8192]{2,1,0:T(8,128)(2,1)}, u32[]{:S(2)}, u32[]{:S(2)}) collective-permute-start(bf16[2,64,8192]{2,1,0:T(8,128)(2,1)} %get-tuple-element.16), channel_id=1, source_target_pairs={{0,31},{1,0},{2,1},{3,2},{4,3},{5,4},{6,5},{7,6},{8,7},{9,8},{10,9... | collective-permute-start | bytes 6291464 | tf_op jit(solution)/shard_map/ppermute | solution.py:13
  203.2 257.0 %collective-permute-start.1 = (bf16[2,64,8192]{2,1,0:T(8,128)(2,1)}, bf16[2,64,8192]{2,1,0:T(8,128)(2,1)}, u32[]{:S(2)}, u32[]{:S(2)}) collective-permute-start(bf16[2,64,8192]{2,1,0:T(8,128)(2,1)} %get-tuple-element.18), channel_id=1, source_target_pairs={{0,29},{1,30},{2,31},{3,0},{4,1},{5,2},{6,3},{7,4},{8,5},{9,6},{10... | collective-permute-start | bytes 6291464 | tf_op jit(solution)/shard_map/ppermute | solution.py:13
  334.6 145.2 %all-to-all-start = ((bf16[8,2,65536]{2,1,0:T(2,128)(2,1)}), bf16[8,2,65536]{2,1,0:T(2,128)(2,1)S(1)}, u32[]{:S(2)}, u32[]{:S(2)}) async-start(bf16[8,2,65536]{2,1,0:T(2,128)(2,1)} %reshape.164), calls=%async_computation.1 | async-start | bytes 4194304 | tf_op jit(solution)/shard_map/all_to_all | solution.py:132
  343.7 2.9 copy-start.2
  469.8 5.7 %copy-start.3 = (bf16[64,8192]{1,0:T(8,128)(2,1)S(1)}, bf16[64,8192]{1,0:T(8,128)(2,1)}, u32[]{:S(2)}) copy-start(bf16[64,8192]{1,0:T(8,128)(2,1)} %get-tuple-element.12) | copy-start | bytes 3145732
Sparse Core Ops, SparseCore 0:
  176.2 55.9 reduce-scatter.1

commit v7 on v6

--- a/solution.py
+++ b/solution.py
@@ -53,7 +53,12 @@
 
     both_blocks = jnp.stack([token_blocks, grad_blocks], axis=1)
     sent_list = [slot_of(both_blocks, k) for k in range(reach_count)]
+    dp_count = lax.axis_size("dp")
+    shard_width = feat_width // dp_count
     pay_list = list(sent_list)
+    pay_list[-1] = jnp.transpose(
+        sent_list[-1].reshape(2, seg_rows, dp_count, shard_width), (2, 0, 1, 3)
+    )
     for k in range(1, reach_count):
         pay_list[k] = shifted(pay_list[k], "adapter", k)
 
@@ -128,11 +133,41 @@
     )
     summed = lax.psum_scatter(joined, "dp", scatter_dimension=0, tiled=True)
     late = pay_list[-1]
-    late_right = right_blocks(late[None], arrived_sel[-1])[0]
-    late_rows = lax.all_to_all(late, "dp", 2, 0, tiled=True)
-    late_right_all = lax.all_gather(late_right, "dp", axis=0, tiled=True)
+    late_sel = arrived_sel[-1].astype(jnp.float32)
+    late_picks = (late_sel[:, None] == jnp.arange(held_count, dtype=jnp.float32)[None, :]).astype(
+        jnp.float32
+    )
+    late_mask = jnp.repeat(late_picks, rank_size, axis=1)
+    late_hidden = (
+        jnp.einsum(
+            "pjd,pdc->jc",
+            late[:, 0],
+            down_cat.reshape(dp_count, shard_width, held_count * rank_size),
+            preferred_element_type=jnp.float32,
+        )
+        * late_mask
+    ).astype(jnp.bfloat16)
+    late_grad = adapter_scale * jnp.einsum(
+        "pjd,cpd->jc",
+        late[:, 1],
+        up_weight_joined.reshape(held_count * rank_size, dp_count, shard_width),
+        preferred_element_type=jnp.float32,
+    )
+    late_grad = (late_grad * late_mask).astype(jnp.bfloat16)
+    late_zero = jnp.zeros_like(late_grad)
+    late_doubled = (adapter_scale * late_hidden.astype(jnp.float32)).astype(jnp.bfloat16)
+    late_right = jnp.stack(
+        [
+            jnp.concatenate([late_grad, late_zero], axis=-1),
+            jnp.concatenate([late_zero, late_doubled], axis=-1),
+        ]
+    )
+    late_spread = jnp.broadcast_to(late_right[None], (dp_count,) + late_right.shape)
+    late_rows_got = lax.all_to_all(late, "dp", 0, 0, tiled=True)
+    late_rows_got, late_spread = lax.optimization_barrier((late_rows_got, late_spread))
+    late_right_got = lax.all_to_all(late_spread, "dp", 0, 0, tiled=True)
     summed = summed + jnp.einsum(
-        "mjd,mjc->dc", late_rows, late_right_all, preferred_element_type=jnp.float32
+        "pwjd,pwjc->dc", late_rows_got, late_right_got, preferred_element_type=jnp.float32
     )
     width = held_count * rank_size
     part_rows = summed.shape[0]

time: 515 us -> 513 us (level)
  waiting for transfers between devices: 184 us -> 220 us
  blocking collectives: 28.8 us -> 0 us
  local copies, waits for them, and re-layouts: 35.1 us -> 18.9 us
  starting transfers between devices: 159 us -> 168 us
    ppermute x9, waiting for transfers between devices: 184 us -> 216 us  [shifted(): return lax.ppermute(value, axis, pairs)]
    all_gather x1 -> x0, blocking collectives: 28.8 us -> none  [on_device(): late_right_all = lax.all_gather(late_right, 'dp', axis=0, tiled=True)]
    all_to_all x1 -> x2, starting transfers between devices: 9.15 us -> 18.8 us  [the longest x1 11.4 us: on_device(): late_right_got = lax.all_to_all(late_spread, 'dp', 0, 0, tiled=True)]
    all_to_all x1 -> x0, local copies, waits for them, and re-layouts: 9.09 us -> none  [on_device(): late_rows = lax.all_to_all(late, 'dp', 2, 0, tiled=True)]
    dot_general x1 -> x3, matrix products: 1.78 us -> 10.4 us  [the longest x1 4.48 us: on_device(): jnp.einsum('pjd,pdc->jc', late[:, 0], down_cat.reshape(dp_count, shard_wi...]
    ppermute x1, local copies, waits for them, and re-layouts: 9.48 us -> 3.13 us  [shifted(): return lax.ppermute(value, axis, pairs)]
    unnamed x10 -> x19, local copies, waits for them, and re-layouts: 13.2 us -> 9.06 us
  transfers between devices with their start and end apart: 11 -> 12, of which waited for: 3 -> 4; matrix products, arithmetic and copies ran while one was open for 17% -> 14% of each run, Pallas kernels for 0% -> 0%
where the time goes in v7:
time: 513 us; the launch traced here: 509 us
  waiting for transfers between devices  220 us (43%)
  starting transfers between devices  168 us (33%)
  matrix products  51.9 us (10%)
  between operations  26.9 us (5%)
  other arithmetic  23 us (4%)
  local copies, waits for them, and re-layouts  18.9 us (4%)
    ppermute x9, waiting for transfers between devices, shifted(): return lax.ppermute(value, axis, pairs)  216 us
    ppermute x9, starting transfers between devices, shifted(): return lax.ppermute(value, axis, pairs)  149 us
    dot_general x4, matrix products, on_device(): jnp.dot(hidden, panels[1], preferred_element_type=jnp.float32)  17.5 us
    dot_general x4, matrix products, on_device(): jnp.dot(hidden_grad, panels[0], preferred_element_type=jnp.float32)  16.3 us
    all_to_all x1, starting transfers between devices, on_device(): late_right_got = lax.all_to_all(late_spread, 'dp', 0, 0, tiled=True)  11.4 us
  transfers between devices with their start and end apart: 12, of which 4 were waited for; matrix products, arithmetic and copies ran while one was open for 14% of the time, Pallas kernels for 0%

profile of v7, /device:TPU:71, one launch (start us, length us, event | category | flops | bytes accessed | tf_op | source)
XLA Modules:
  0.0 508.6 jit_solution(16873816063462343331)
XLA Ops:
  7.2 0.7 multiply_subtract_fusion
  7.9 0.6 fusion.66
  13.7 2.4 select_select_fusion
  16.1 2.9 select_select_fusion.1
  18.9 4.2 collective-permute-start.7
  23.1 0.7 collective-permute-start.6
  23.9 0.6 fusion.65
  25.8 132.4 %collective-permute-start.4 = (s32[1]{0:T(128)}, s32[1]{0:T(128)}, u32[]{:S(2)}, u32[]{:S(2)}) collective-permute-start(s32[1]{0:T(128)} %bitcast.26), channel_id=1, source_target_pairs={{0,1},{1,2},{2,3},{3,4},{4,5},{5,6},{6,7},{7,8},{8,9},{9,10},{10,1... | collective-permute-start | bytes 20 | tf_op jit(solution)/shard_map/ppermute | solution.py:13
  159.4 1.5 collective-permute-start.2
  162.3 0.5 collective-permute-done.2
  162.8 1.3 add_convert_fusion.1
  164.3 0.1 mul.86
  164.4 3.3 pad_maximum_fusion
  167.7 1.0 fusion.18
  168.8 0.6 copy-done.2
  169.3 1.0 fusion.19
  170.4 5.7 %convolution_bitcast_fusion = f32[8192,256]{1,0:T(8,128)} fusion(bf16[3,2,64,8192]{3,2,0,1:T(8,128)(2,1)S(1)} %pad_maximum_fusion, bf16[3,1,64,256]{3,2,0,1:T(8,128)(2,1)S(1)} %get-tuple-element.32, bf16[3,1,64,256]{3,2,0,1:T(8,128)(2,1)S(1)} %get-tuple-element.33), kind=kOutput, calls=%fused_computation | convolution fusion | flops 1610711040 | bytes 14876672 | tf_op jit(solution)/shard_map/nwjd,nwjc->dc/dot_general | solution.py:131
  177.3 3.7 collective-permute-start
  181.1 3.0 copy.50
  184.1 2.5 copy.80
  186.6 2.5 collective-permute-start.8
  189.1 4.1 broadcast_select_fusion
  195.0 3.0 select_bitcast_fusion
  198.0 2.7 copy.52
  200.7 2.7 copy.51
  203.5 3.9 fusion.3
  207.3 4.0 collective-permute-start.5
  211.4 2.9 convolution_convert_fusion
  215.1 107.9 %collective-permute-done.8 = bf16[8,2,64,1024]{3,2,0,1:T(8,128)(2,1)} collective-permute-done((bf16[8,2,64,1024]{3,2,0,1:T(8,128)(2,1)}, bf16[8,2,64,1024]{3,2,0,1:T(8,128)(2,1)}, u32[]{:S(2)}, u32[]{:S(2)}) %collective-permute-start.8) | collective-permute-done | bytes 2097184 | tf_op jit(solution)/shard_map/ppermute | solution.py:13
  323.0 3.1 copy.39
  326.1 7.3 %all-to-all-start = ((bf16[8,2,64,1024]{3,2,1,0:T(8,128)(2,1)}), bf16[8,2,64,1024]{3,2,1,0:T(8,128)(2,1)}, u32[]{:S(2)}, u32[]{:S(2)}) async-start(bf16[8,2,64,1024]{3,2,1,0:T(8,128)(2,1)} %copy.39), calls=%async_computation.1 | async-start | bytes 4194304 | tf_op jit(solution)/shard_map/all_to_all | solution.py:166
  333.5 4.5 fusion.44
  337.9 3.6 fusion.32
  341.6 4.2 fusion.1
  345.8 4.1 convolution_convert_fusion.2
  349.9 4.1 fusion.2
  354.1 4.3 convolution_convert_fusion.1
  358.4 107.5 %collective-permute-done.1 = bf16[2,64,8192]{2,1,0:T(8,128)(2,1)} collective-permute-done((bf16[2,64,8192]{2,1,0:T(8,128)(2,1)}, bf16[2,64,8192]{2,1,0:T(8,128)(2,1)}, u32[]{:S(2)}, u32[]{:S(2)}) %collective-permute-start.1) | collective-permute-done | bytes 2097184 | tf_op jit(solution)/shard_map/ppermute | solution.py:13
  466.0 4.9 select_select_fusion.5
  470.9 5.4 %select_select_fusion.7 = (bf16[64,8192]{1,0:T(8,128)(2,1)}, bf16[64,8192]{1,0:T(8,128)(2,1)}) fusion(bf16[64,8192]{1,0:T(8,128)(2,1)} %fusion.1, bf16[64,8192]{1,0:T(8,128)(2,1)} %fusion.2, bf16[64,8192]{1,0:T(8,128)(2,1)} %fusion.3, pred[]{:T(512)} %bitcast.23, pred[]{:T(512)} %bitcast.15, pred[]{:T(512)} %bitcast, pred[]{:T(512)} %bitcast.24, ...), kind=kOutput, calls=%fused_computation.93 | convolution fusion | flops 138416128 | bytes 8388614 | tf_op jit(solution)/shard_map/dot_general | solution.py:85
  476.3 0.9 broadcast_in_dim.11
  477.2 11.4 %all-to-all-start.1 = ((bf16[8,2,64,256]{3,2,1,0:T(8,128)(2,1)}), bf16[8,2,64,256]{3,2,1,0:T(8,128)(2,1)S(1)}, u32[]{:S(2)}, u32[]{:S(2)}) async-start(bf16[8,2,64,256]{3,2,1,0:T(8,128)(2,1)} %broadcast_in_dim.11), calls=%async_computation.2 | async-start | bytes 1048576 | tf_op jit(solution)/shard_map/all_to_all | solution.py:168
  488.6 3.9 pad_maximum_fusion.3
  492.5 3.7 all-to-all-done.1
  496.3 2.3 convolution_bitcast_fusion.1
  498.6 1.3 add_convert_fusion
  500.0 0.8 copy.43
  500.9 0.8 copy.44
  (39 shorter events, 0.6 us)
Async XLA Ops:
  7.2 491.5 %reduce-scatter.2.cloned.1.call-start = ((), (), s32[]{:S(2)}) async-start(), calls=%async_computation.3 | async-start | bytes 9437184 | tf_op jit(solution)/shard_map/reduce_scatter | solution.py:134
  18.9 145.4 %collective-permute-start.7 = (bf16[2,64,8192]{2,1,0:T(8,128)(2,1)}, bf16[2,64,8192]{2,1,0:T(8,128)(2,1)}, u32[]{:S(2)}, u32[]{:S(2)}) collective-permute-start(bf16[2,64,8192]{2,1,0:T(8,128)(2,1)} %bitcast.44), channel_id=1, source_target_pairs={{0,2},{1,3},{2,4},{3,5},{4,6},{5,7},{6,8},{7,9},{8,10},{9,11},{10,... | collective-permute-start | bytes 6291464 | tf_op jit(solution)/shard_map/ppermute | solution.py:13
  23.1 141.2 %collective-permute-start.6 = (bf16[2,64,8192]{2,1,0:T(8,128)(2,1)}, bf16[2,64,8192]{2,1,0:T(8,128)(2,1)}, u32[]{:S(2)}, u32[]{:S(2)}) collective-permute-start(bf16[2,64,8192]{2,1,0:T(8,128)(2,1)} %bitcast.41), channel_id=1, source_target_pairs={{0,1},{1,2},{2,3},{3,4},{4,5},{5,6},{6,7},{7,8},{8,9},{9,10},{10,1... | collective-permute-start | bytes 6291464 | tf_op jit(solution)/shard_map/ppermute | solution.py:13
  25.8 136.5 %collective-permute-start.4 = (s32[1]{0:T(128)}, s32[1]{0:T(128)}, u32[]{:S(2)}, u32[]{:S(2)}) collective-permute-start(s32[1]{0:T(128)} %bitcast.26), channel_id=1, source_target_pairs={{0,1},{1,2},{2,3},{3,4},{4,5},{5,6},{6,7},{7,8},{8,9},{9,10},{10,1... | collective-permute-start | bytes 20 | tf_op jit(solution)/shard_map/ppermute | solution.py:13
  159.4 3.3 collective-permute-start.2
  164.4 3.4 copy-start
  167.7 1.6 copy-start.2
  177.3 17.0 %collective-permute-start = (s32[1]{0:T(128)}, s32[1]{0:T(128)}, u32[]{:S(2)}, u32[]{:S(2)}) collective-permute-start(s32[1]{0:T(128)} %bitcast.7), channel_id=1, source_target_pairs={{0,3},{1,4},{2,5},{3,6},{4,7},{5,8},{6,9},{7,10},{8,11},{9,12},{10... | collective-permute-start | bytes 20 | tf_op jit(solution)/shard_map/ppermute | solution.py:13
  186.6 136.4 %collective-permute-start.8 = (bf16[8,2,64,1024]{3,2,0,1:T(8,128)(2,1)}, bf16[8,2,64,1024]{3,2,0,1:T(8,128)(2,1)}, u32[]{:S(2)}, u32[]{:S(2)}) collective-permute-start(bf16[8,2,64,1024]{3,2,0,1:T(8,128)(2,1)} %bitcast.212), channel_id=1, source_target_pairs={{0,3},{1,4},{2,5},{3,6},{4,7},{5,8},{6,9},{7,10},{8,11},{9,12},{10... | collective-permute-start | bytes 6291464 | tf_op jit(solution)/shard_map/ppermute | solution.py:13
  195.0 3.0 copy-start.1
  198.0 143.7 %collective-permute-start.3 = (bf16[2,64,8192]{2,1,0:T(8,128)(2,1)}, bf16[2,64,8192]{2,1,0:T(8,128)(2,1)}, u32[]{:S(2)}, u32[]{:S(2)}) collective-permute-start(bf16[2,64,8192]{2,1,0:T(8,128)(2,1)} %get-tuple-element.21), channel_id=1, source_target_pairs={{0,30},{1,31},{2,0},{3,1},{4,2},{5,3},{6,4},{7,5},{8,6},{9,7},{10,... | collective-permute-start | bytes 6291464 | tf_op jit(solution)/shard_map/ppermute | solution.py:13
  198.0 2.7 copy-start.3
  207.3 142.6 %collective-permute-start.5 = (bf16[2,64,8192]{2,1,0:T(8,128)(2,1)}, bf16[2,64,8192]{2,1,0:T(8,128)(2,1)}, u32[]{:S(2)}, u32[]{:S(2)}) collective-permute-start(bf16[2,64,8192]{2,1,0:T(8,128)(2,1)} %get-tuple-element.20), channel_id=1, source_target_pairs={{0,31},{1,0},{2,1},{3,2},{4,3},{5,4},{6,5},{7,6},{8,7},{9,8},{10,9... | collective-permute-start | bytes 6291464 | tf_op jit(solution)/shard_map/ppermute | solution.py:13
  214.3 251.7 %collective-permute-start.1 = (bf16[2,64,8192]{2,1,0:T(8,128)(2,1)}, bf16[2,64,8192]{2,1,0:T(8,128)(2,1)}, u32[]{:S(2)}, u32[]{:S(2)}) collective-permute-start(bf16[2,64,8192]{2,1,0:T(8,128)(2,1)} %get-tuple-element.22), channel_id=1, source_target_pairs={{0,29},{1,30},{2,31},{3,0},{4,1},{5,2},{6,3},{7,4},{8,5},{9,6},{10... | collective-permute-start | bytes 6291464 | tf_op jit(solution)/shard_map/ppermute | solution.py:13
  326.1 150.1 %all-to-all-start = ((bf16[8,2,64,1024]{3,2,1,0:T(8,128)(2,1)}), bf16[8,2,64,1024]{3,2,1,0:T(8,128)(2,1)}, u32[]{:S(2)}, u32[]{:S(2)}) async-start(bf16[8,2,64,1024]{3,2,1,0:T(8,128)(2,1)} %copy.39), calls=%async_computation.1 | async-start | bytes 4194304 | tf_op jit(solution)/shard_map/all_to_all | solution.py:166
  333.5 4.5 copy-start.5
  354.1 111.9 %copy-start.4 = (bf16[1,2,64,8192]{3,2,1,0:T(8,128)(2,1)S(1)}, bf16[1,2,64,8192]{3,2,1,0:T(8,128)(2,1)}, u32[]{:S(2)}) copy-start(bf16[1,2,64,8192]{3,2,1,0:T(8,128)(2,1)} %get-tuple-element.25) | copy-start | bytes 6291460
  470.9 17.7 %copy-start.7 = (bf16[64,8192]{1,0:T(8,128)(2,1)S(1)}, bf16[64,8192]{1,0:T(8,128)(2,1)}, u32[]{:S(2)}) copy-start(bf16[64,8192]{1,0:T(8,128)(2,1)} %get-tuple-element.17) | copy-start | bytes 3145732
  476.2 12.4 %copy-start.6 = (bf16[64,8192]{1,0:T(8,128)(2,1)S(1)}, bf16[64,8192]{1,0:T(8,128)(2,1)}, u32[]{:S(2)}) copy-start(bf16[64,8192]{1,0:T(8,128)(2,1)} %get-tuple-element.16) | copy-start | bytes 3145732
  477.2 19.1 %all-to-all-start.1 = ((bf16[8,2,64,256]{3,2,1,0:T(8,128)(2,1)}), bf16[8,2,64,256]{3,2,1,0:T(8,128)(2,1)S(1)}, u32[]{:S(2)}, u32[]{:S(2)}) async-start(bf16[8,2,64,256]{3,2,1,0:T(8,128)(2,1)} %broadcast_in_dim.11), calls=%async_computation.2 | async-start | bytes 1048576 | tf_op jit(solution)/shard_map/all_to_all | solution.py:168
Sparse Core Ops, SparseCore 0:
  176.2 55.9 reduce-scatter.1

commit v8 on v7

--- a/solution.py
+++ b/solution.py
@@ -162,12 +162,15 @@
             jnp.concatenate([late_zero, late_doubled], axis=-1),
         ]
     )
-    late_spread = jnp.broadcast_to(late_right[None], (dp_count,) + late_right.shape)
-    late_rows_got = lax.all_to_all(late, "dp", 0, 0, tiled=True)
-    late_rows_got, late_spread = lax.optimization_barrier((late_rows_got, late_spread))
-    late_right_got = lax.all_to_all(late_spread, "dp", 0, 0, tiled=True)
+    late_pack = jnp.concatenate(
+        [late, jnp.broadcast_to(late_right[None], (dp_count,) + late_right.shape)], axis=-1
+    )
+    late_got = lax.all_to_all(late_pack, "dp", 0, 0, tiled=True)
     summed = summed + jnp.einsum(
-        "pwjd,pwjc->dc", late_rows_got, late_right_got, preferred_element_type=jnp.float32
+        "pwjd,pwjc->dc",
+        late_got[..., :shard_width],
+        late_got[..., shard_width:],
+        preferred_element_type=jnp.float32,
     )
     width = held_count * rank_size
     part_rows = summed.shape[0]

time: 513 us -> 507 us (0.988)
  starting transfers between devices: 168 us -> 157 us
    all_to_all x2 -> x1, starting transfers between devices: 18.8 us -> 7.93 us  [on_device(): late_got = lax.all_to_all(late_pack, 'dp', 0, 0, tiled=True)]
    ppermute x9, waiting for transfers between devices: 216 us -> 221 us  [shifted(): return lax.ppermute(value, axis, pairs)]
    unnamed x19 -> x17, local copies, waits for them, and re-layouts: 9.06 us -> 11.5 us
  transfers between devices with their start and end apart: 12 -> 11, of which waited for: 4 -> 3; matrix products, arithmetic and copies ran while one was open for 14% -> 15% of each run, Pallas kernels for 0% -> 0%
where the time goes in v8:
time: 507 us; the launch traced here: 499 us
  waiting for transfers between devices  221 us (44%)
  starting transfers between devices  157 us (31%)
  matrix products  51.9 us (10%)
  between operations  26.9 us (5%)
  other arithmetic  22.7 us (4%)
  local copies, waits for them, and re-layouts  19.2 us (4%)
    ppermute x9, waiting for transfers between devices, shifted(): return lax.ppermute(value, axis, pairs)  221 us
    ppermute x9, starting transfers between devices, shifted(): return lax.ppermute(value, axis, pairs)  149 us
    dot_general x4, matrix products, on_device(): jnp.dot(hidden, panels[1], preferred_element_type=jnp.float32)  17.6 us
    dot_general x4, matrix products, on_device(): jnp.dot(hidden_grad, panels[0], preferred_element_type=jnp.float32)  16.2 us
    unnamed x17, local copies, waits for them, and re-layouts  11.5 us
  transfers between devices with their start and end apart: 11, of which 3 were waited for; matrix products, arithmetic and copies ran while one was open for 15% of the time, Pallas kernels for 0%

profile of v8, /device:TPU:71, one launch (start us, length us, event | category | flops | bytes accessed | tf_op | source)
XLA Modules:
  0.0 499.2 jit_solution(3337350413706820994)
XLA Ops:
  7.2 0.7 multiply_subtract_fusion
  7.9 0.6 fusion.72
  13.7 2.4 select_select_fusion
  16.1 2.9 select_select_fusion.1
  18.9 4.2 collective-permute-start.7
  23.1 0.7 collective-permute-start.6
  23.9 0.6 fusion.71
  25.8 132.4 %collective-permute-start.4 = (s32[1]{0:T(128)}, s32[1]{0:T(128)}, u32[]{:S(2)}, u32[]{:S(2)}) collective-permute-start(s32[1]{0:T(128)} %bitcast.26), channel_id=1, source_target_pairs={{0,1},{1,2},{2,3},{3,4},{4,5},{5,6},{6,7},{7,8},{8,9},{9,10},{10,1... | collective-permute-start | bytes 20 | tf_op jit(solution)/shard_map/ppermute | solution.py:13
  159.4 1.5 collective-permute-start.2
  162.3 0.5 collective-permute-done.2
  162.8 1.3 add_convert_fusion.1
  164.2 0.1 mul.86
  164.3 3.3 pad_maximum_fusion
  167.7 1.0 fusion.23
  168.7 0.6 copy-done
  169.3 1.0 fusion.24
  170.3 5.7 %convolution_bitcast_fusion = f32[8192,256]{1,0:T(8,128)} fusion(bf16[3,2,64,8192]{3,2,0,1:T(8,128)(2,1)S(1)} %pad_maximum_fusion, bf16[3,1,64,256]{3,2,0,1:T(8,128)(2,1)S(1)} %get-tuple-element.28, bf16[3,1,64,256]{3,2,0,1:T(8,128)(2,1)S(1)} %get-tuple-element.29), kind=kOutput, calls=%fused_computation | convolution fusion | flops 1610711040 | bytes 14876672 | tf_op jit(solution)/shard_map/nwjd,nwjc->dc/dot_general | solution.py:131
  177.3 3.7 collective-permute-start
  181.0 3.0 copy.52
  184.0 2.5 copy.82
  186.5 2.5 collective-permute-start.8
  189.0 5.1 %copy.54 = bf16[16,8,8,1024]{3,2,1,0:T(8,128)(2,1)} copy(bf16[16,8,8,1024]{3,1,2,0:T(8,128)(2,1)} %bitcast.216) | data formatting | bytes 4194304
  194.1 2.8 copy.53
  196.9 1.5 broadcast_select_fusion
  200.2 3.0 select_bitcast_fusion
  203.3 3.9 fusion.3
  207.2 2.9 convolution_convert_fusion
  210.1 3.8 collective-permute-start.5
  213.9 0.4 collective-permute-start.1
  215.0 0.1 broadcast_in_dim.10
  215.1 107.3 %collective-permute-done.8 = bf16[8,2,64,1024]{3,2,0,1:T(8,128)(2,1)} collective-permute-done((bf16[8,2,64,1024]{3,2,0,1:T(8,128)(2,1)}, bf16[8,2,64,1024]{3,2,0,1:T(8,128)(2,1)}, u32[]{:S(2)}, u32[]{:S(2)}) %collective-permute-start.8) | collective-permute-done | bytes 2097184 | tf_op jit(solution)/shard_map/ppermute | solution.py:13
  322.4 4.3 fusion.49
  326.7 3.6 fusion.37
  330.5 1.8 pad_maximum_fusion.1
  332.3 1.8 copy.43
  334.1 7.9 %all-to-all-start = ((bf16[8,2,64,1280]{3,2,1,0:T(8,128)(2,1)}), bf16[8,2,64,1280]{3,2,1,0:T(8,128)(2,1)}, u32[]{:S(2)}, u32[]{:S(2)}) async-start(bf16[8,2,64,1280]{3,2,1,0:T(8,128)(2,1)} %copy.43), calls=%async_computation.1 | async-start | bytes 5242880 | tf_op jit(solution)/shard_map/all_to_all | solution.py:168
  342.1 4.2 fusion.1
  346.2 4.1 convolution_convert_fusion.2
  350.4 4.1 fusion.2
  354.5 4.3 convolution_convert_fusion.1
  358.8 113.4 %collective-permute-done.1 = bf16[2,64,8192]{2,1,0:T(8,128)(2,1)} collective-permute-done((bf16[2,64,8192]{2,1,0:T(8,128)(2,1)}, bf16[2,64,8192]{2,1,0:T(8,128)(2,1)}, u32[]{:S(2)}, u32[]{:S(2)}) %collective-permute-start.1) | collective-permute-done | bytes 2097184 | tf_op jit(solution)/shard_map/ppermute | solution.py:13
  472.2 4.9 select_select_fusion.5
  477.1 5.4 %select_select_fusion.7 = (bf16[64,8192]{1,0:T(8,128)(2,1)}, bf16[64,8192]{1,0:T(8,128)(2,1)}) fusion(bf16[64,8192]{1,0:T(8,128)(2,1)} %fusion.1, bf16[64,8192]{1,0:T(8,128)(2,1)} %fusion.2, bf16[64,8192]{1,0:T(8,128)(2,1)} %fusion.3, pred[]{:T(512)} %bitcast.23, pred[]{:T(512)} %bitcast.15, pred[]{:T(512)} %bitcast, pred[]{:T(512)} %bitcast.24, ...), kind=kOutput, calls=%fused_computation.96 | convolution fusion | flops 138416128 | bytes 8388614 | tf_op jit(solution)/shard_map/dot_general | solution.py:85
  482.5 4.3 pad_maximum_fusion.4
  486.8 2.4 fusion.15
  489.2 1.3 add_convert_fusion
  490.6 0.8 copy.45
  491.5 0.8 copy.46
  (36 shorter events, 0.5 us)
Async XLA Ops:
  7.2 482.1 %reduce-scatter.2.cloned.1.call-start = ((), (), s32[]{:S(2)}) async-start(), calls=%async_computation.2 | async-start | bytes 9437184 | tf_op jit(solution)/shard_map/reduce_scatter | solution.py:134
  18.9 145.4 %collective-permute-start.7 = (bf16[2,64,8192]{2,1,0:T(8,128)(2,1)}, bf16[2,64,8192]{2,1,0:T(8,128)(2,1)}, u32[]{:S(2)}, u32[]{:S(2)}) collective-permute-start(bf16[2,64,8192]{2,1,0:T(8,128)(2,1)} %bitcast.44), channel_id=1, source_target_pairs={{0,2},{1,3},{2,4},{3,5},{4,6},{5,7},{6,8},{7,9},{8,10},{9,11},{10,... | collective-permute-start | bytes 6291464 | tf_op jit(solution)/shard_map/ppermute | solution.py:13
  23.1 141.2 %collective-permute-start.6 = (bf16[2,64,8192]{2,1,0:T(8,128)(2,1)}, bf16[2,64,8192]{2,1,0:T(8,128)(2,1)}, u32[]{:S(2)}, u32[]{:S(2)}) collective-permute-start(bf16[2,64,8192]{2,1,0:T(8,128)(2,1)} %bitcast.41), channel_id=1, source_target_pairs={{0,1},{1,2},{2,3},{3,4},{4,5},{5,6},{6,7},{7,8},{8,9},{9,10},{10,1... | collective-permute-start | bytes 6291464 | tf_op jit(solution)/shard_map/ppermute | solution.py:13
  25.8 136.5 %collective-permute-start.4 = (s32[1]{0:T(128)}, s32[1]{0:T(128)}, u32[]{:S(2)}, u32[]{:S(2)}) collective-permute-start(s32[1]{0:T(128)} %bitcast.26), channel_id=1, source_target_pairs={{0,1},{1,2},{2,3},{3,4},{4,5},{5,6},{6,7},{7,8},{8,9},{9,10},{10,1... | collective-permute-start | bytes 20 | tf_op jit(solution)/shard_map/ppermute | solution.py:13
  159.4 3.3 collective-permute-start.2
  164.3 3.4 copy-start.2
  167.7 1.6 copy-start
  177.3 22.3 %collective-permute-start = (s32[1]{0:T(128)}, s32[1]{0:T(128)}, u32[]{:S(2)}, u32[]{:S(2)}) collective-permute-start(s32[1]{0:T(128)} %bitcast.7), channel_id=1, source_target_pairs={{0,3},{1,4},{2,5},{3,6},{4,7},{5,8},{6,9},{7,10},{8,11},{9,12},{10... | collective-permute-start | bytes 20 | tf_op jit(solution)/shard_map/ppermute | solution.py:13
  186.5 135.9 %collective-permute-start.8 = (bf16[8,2,64,1024]{3,2,0,1:T(8,128)(2,1)}, bf16[8,2,64,1024]{3,2,0,1:T(8,128)(2,1)}, u32[]{:S(2)}, u32[]{:S(2)}) collective-permute-start(bf16[8,2,64,1024]{3,2,0,1:T(8,128)(2,1)} %bitcast.210), channel_id=1, source_target_pairs={{0,3},{1,4},{2,5},{3,6},{4,7},{5,8},{6,9},{7,10},{8,11},{9,12},{10... | collective-permute-start | bytes 6291464 | tf_op jit(solution)/shard_map/ppermute | solution.py:13
  189.0 5.1 %copy-start.1 = (bf16[2,64,8192]{2,1,0:T(8,128)(2,1)S(1)}, bf16[2,64,8192]{2,1,0:T(8,128)(2,1)}, u32[]{:S(2)}) copy-start(bf16[2,64,8192]{2,1,0:T(8,128)(2,1)} %param.8) | copy-start | bytes 6291460
  194.1 2.8 copy-start.3
  203.3 138.8 %collective-permute-start.3 = (bf16[2,64,8192]{2,1,0:T(8,128)(2,1)}, bf16[2,64,8192]{2,1,0:T(8,128)(2,1)}, u32[]{:S(2)}, u32[]{:S(2)}) collective-permute-start(bf16[2,64,8192]{2,1,0:T(8,128)(2,1)} %get-tuple-element.17), channel_id=1, source_target_pairs={{0,30},{1,31},{2,0},{3,1},{4,2},{5,3},{6,4},{7,5},{8,6},{9,7},{10,... | collective-permute-start | bytes 6291464 | tf_op jit(solution)/shard_map/ppermute | solution.py:13
  210.1 116.7 %copy-start.5 = (bf16[16,8,8,1024]{3,2,1,0:T(8,128)(2,1)S(1)}, bf16[16,8,8,1024]{3,2,1,0:T(8,128)(2,1)}, u32[]{:S(2)}) copy-start(bf16[16,8,8,1024]{3,2,1,0:T(8,128)(2,1)} %copy.53) | copy-start | bytes 6291460
  210.1 140.3 %collective-permute-start.5 = (bf16[2,64,8192]{2,1,0:T(8,128)(2,1)}, bf16[2,64,8192]{2,1,0:T(8,128)(2,1)}, u32[]{:S(2)}, u32[]{:S(2)}) collective-permute-start(bf16[2,64,8192]{2,1,0:T(8,128)(2,1)} %get-tuple-element.16), channel_id=1, source_target_pairs={{0,31},{1,0},{2,1},{3,2},{4,3},{5,4},{6,5},{7,6},{8,7},{9,8},{10,9... | collective-permute-start | bytes 6291464 | tf_op jit(solution)/shard_map/ppermute | solution.py:13
  213.9 258.3 %collective-permute-start.1 = (bf16[2,64,8192]{2,1,0:T(8,128)(2,1)}, bf16[2,64,8192]{2,1,0:T(8,128)(2,1)}, u32[]{:S(2)}, u32[]{:S(2)}) collective-permute-start(bf16[2,64,8192]{2,1,0:T(8,128)(2,1)} %get-tuple-element.18), channel_id=1, source_target_pairs={{0,29},{1,30},{2,31},{3,0},{4,1},{5,2},{6,3},{7,4},{8,5},{9,6},{10... | collective-permute-start | bytes 6291464 | tf_op jit(solution)/shard_map/ppermute | solution.py:13
  334.1 152.7 %all-to-all-start = ((bf16[8,2,64,1280]{3,2,1,0:T(8,128)(2,1)}), bf16[8,2,64,1280]{3,2,1,0:T(8,128)(2,1)}, u32[]{:S(2)}, u32[]{:S(2)}) async-start(bf16[8,2,64,1280]{3,2,1,0:T(8,128)(2,1)} %copy.43), calls=%async_computation.1 | async-start | bytes 5242880 | tf_op jit(solution)/shard_map/all_to_all | solution.py:168
  354.5 117.6 %copy-start.4 = (bf16[1,2,64,8192]{3,2,1,0:T(8,128)(2,1)S(1)}, bf16[1,2,64,8192]{3,2,1,0:T(8,128)(2,1)}, u32[]{:S(2)}) copy-start(bf16[1,2,64,8192]{3,2,1,0:T(8,128)(2,1)} %get-tuple-element.21) | copy-start | bytes 6291460
  477.1 5.4 %copy-start.6 = (bf16[64,8192]{1,0:T(8,128)(2,1)S(1)}, bf16[64,8192]{1,0:T(8,128)(2,1)}, u32[]{:S(2)}) copy-start(bf16[64,8192]{1,0:T(8,128)(2,1)} %get-tuple-element.12) | copy-start | bytes 3145732
Sparse Core Ops, SparseCore 0:
  176.1 55.8 reduce-scatter.1
